TPU v7x, 128 devices: a whole 4x4x4 slice. The times are simulated.
128 devices in a mesh: tm: 8 (over y, core), neuron: 8 (over x, z_hi), motif: 2 (over z_lo).
Axes of the slice: x: 4, y: 4, z: 4 (z_hi: 2, z_lo: 2; z = z_hi * 2 + z_lo), core: 2. Of those that a mesh axis runs over, the one named last changes fastest.
Arguments:
- counts: int32 [2048, 8192], P('neuron', 'tm'), may hold values from 0 to 2
- motif_w: float32 [64, 64, 2048], P('motif', None, 'neuron'), may hold values from 0.05 to 3, as said below
- motif_h: float32 [64, 8192], P('motif', 'tm'), may hold values from 0.05 to 3, as said below
Outputs:
- new_w: float32 [64, 64, 2048], P('motif', None, 'neuron')
- new_h: float32 [64, 8192], P('motif', 'tm')
Inputs may be any that keep to these rules, and one draw needn't show every extreme that they name: `motif_w`: positive factors. `motif_h`: positive activations.
All inputs are finite; a program needn't handle non-finite values.
Results may differ from a plain program's by a relative error of at most 0.0003.
Values may be sent and summed in bfloat16 or wider, within the bound.
No kernel may reach another device: no remote copies, remote signals or barrier semaphores. Data moves between devices by JAX's collectives and lax.ppermute only.
A program may use at most 128 MiB of HBM per device.

v0:
```python
import jax
import jax.numpy as jnp
from jax import lax
from jax.sharding import PartitionSpec as P

MOTIFS = 64
LAGS = 64
ITERS = 2


def from_behind(value, axis, steps):
    count = lax.axis_size(axis)
    first, last = (max(0, -steps), min(count, count - steps))
    return lax.ppermute(value, axis, [(source, source + steps) for source in range(first, last)])


def stacked(hext, count, rim, width):
    rows = [hext[:, rim - lag : rim - lag + width] for lag in range(rim + 1)]
    return jnp.stack(rows, axis=1).reshape(count * (rim + 1), width)


def local(counts, motif_w, motif_h):
    k_dev, lags, n_dev = motif_w.shape
    width = counts.shape[1]
    rim = lags - 1
    scale_factor = 1.0 / (MOTIFS * LAGS)
    total_bins = width * lax.axis_size("tm")
    leading_bin = lax.axis_index("tm") * width
    reduce_over_rows = (((0,), (0,)), ((), ()))
    contract_cols = (((1,), (1,)), ((), ()))
    spike_events = counts.astype(jnp.float32)
    weights = motif_w.reshape(k_dev * lags, n_dev)
    weight_bfloat = weights.astype(jnp.bfloat16)
    acts = motif_h

    def extend_padded(acts):
        hbf = acts.astype(jnp.bfloat16)
        before = from_behind(hbf[:, width - rim :], "tm", 1)
        return jnp.concatenate([before, hbf], axis=1)

    def ratio_and_lagged(weight_bfloat, hext):
        lagged_copies = stacked(hext, k_dev, rim, width)
        part = (
            lax.dot_general(
                weight_bfloat, lagged_copies, reduce_over_rows, preferred_element_type=jnp.float32
            )
            * scale_factor
        )
        estimated_counts = lax.psum(part, "motif")
        return ((spike_events / estimated_counts).astype(jnp.bfloat16), lagged_copies)

    bins = leading_bin + jnp.arange(width, dtype=jnp.int32)
    offsets = jnp.arange(lags, dtype=jnp.int32)
    mask = (bins[None, :] + offsets[:, None] < total_bins).astype(jnp.float32)
    hext = extend_padded(acts)
    for step in range(ITERS):
        ratio, lagged_copies = ratio_and_lagged(weight_bfloat, hext)
        after = from_behind(ratio[:, :rim], "tm", -1)
        rext = jnp.concatenate([ratio, after], axis=1)
        prod = jnp.dot(weight_bfloat, rext, preferred_element_type=jnp.float32).reshape(
            k_dev, lags, width + rim
        )
        hnum = jnp.zeros((k_dev, width), jnp.float32)
        for lag in range(lags):
            hnum = hnum + prod[:, lag, lag : lag + width]
        colsum = jnp.sum(weight_bfloat.reshape(k_dev, lags, n_dev), axis=2, dtype=jnp.float32)
        hnum, colsum = lax.psum((hnum, colsum), "neuron")
        hden = jnp.dot(colsum, mask, precision=lax.Precision.HIGHEST)
        acts = acts * hnum / hden
        hext = extend_padded(acts)
        ratio, lagged_copies = ratio_and_lagged(weight_bfloat, hext)
        wnum = lax.dot_general(
            lagged_copies, ratio, contract_cols, preferred_element_type=jnp.float32
        )
        wden = jnp.sum(lagged_copies, axis=1, dtype=jnp.float32)
        wnum, wden = lax.psum((wnum, wden), "tm")
        weights = weights * wnum / wden[:, None]
        weight_bfloat = weights.astype(jnp.bfloat16)
    return (weights.reshape(k_dev, lags, n_dev), acts)


def solution(mesh):
    in_specs = (P("neuron", "tm"), P("motif", None, "neuron"), P("motif", "tm"))
    out_specs = (P("motif", None, "neuron"), P("motif", "tm"))
    return jax.shard_map(local, mesh=mesh, in_specs=in_specs, out_specs=out_specs, check_vma=False)
```

profile of v0, /device:TPU:1, one launch (start us, length us, event | category | flops | bytes accessed | tf_op | source)
XLA Modules:
  0.0 741.4 jit_solution(326624774348713325)
XLA Ops:
  8.2 4.6 collective-permute-start
  59.7 29.5 %stack.714 = bf16[32,64,1024]{2,1,0:T(8,128)(2,1)} concatenate(bf16[32,1,1024]{2,1,0:T(2,128)(2,1)S(1)} %copy.6175, bf16[32,1,1024]{2,1,0:T(2,128)(2,1)S(1)} %copy.6176, bf16[32,1,1024]{2,1,0:T(2,128)(2,1)S(1)} %copy.6177, bf16[32,1,1024]{2,1,0:T(2,128)(2,1)S(1)} %copy.6178, bf16[32,1,1024]{2,1,0:T(2,128)(2,1)S(1)} %copy.6179, bf16[32,1,1024]{2,1,0:T(2,128)(2,1)S(1)} %copy.6180, ...), dimensions={1} | concatenate | bytes 8388608 | tf_op jit(solution)/shard_map/stack | solution.py:19
  89.3 4.5 fusion.2
  94.2 48.0 %all-reduce.9.cloned.1.call-done = f32[256,1024]{0,1:T(8,128)} async-done(((f32[256,1024]{0,1:T(8,128)}), f32[256,1024]{0,1:T(8,128)}) %all-reduce.9.cloned.1.call-update) | async-done | bytes 1048592 | tf_op jit(solution)/shard_map/psum | solution.py:49
  149.1 4.8 convolution_bitcast_fusion
  153.9 9.7 %copy.6239 = f32[2048,1087]{1,0:T(8,128)} copy(f32[2048,1087]{0,1:T(8,128)} %convolution_bitcast_fusion) | data formatting | bytes 17809408 | tf_op jit(solution)/shard_map/dot_general | solution.py:60
  163.6 12.2 %fusion.403 = (f32[32,1,1024]{2,1,0:T(1,128)S(1)}, f32[32,1,1024]{2,1,0:T(1,128)S(1)}, f32[32,1,1024]{2,1,0:T(1,128)S(1)}, f32[32,1,1024]{2,1,0:T(1,128)S(1)}, f...) fusion(f32[32,64,1087]{2,1,0:T(8,128)} %bitcast.1062), kind=kLoop, calls=%fused_computation.865 | loop fusion | bytes 4980736 | tf_op jit(solution)/shard_map/slice | solution.py:65
  175.9 11.8 %fusion.404 = (f32[32,1,1024]{2,1,0:T(1,128)S(1)}, f32[32,1,1024]{2,1,0:T(1,128)S(1)}, f32[32,1,1024]{2,1,0:T(1,128)S(1)}, f32[32,1,1024]{2,1,0:T(1,128)S(1)}, f...) fusion(f32[32,64,1087]{2,1,0:T(8,128)} %bitcast.1063), kind=kLoop, calls=%fused_computation.866 | loop fusion | bytes 4980736 | tf_op jit(solution)/shard_map/slice | solution.py:65
  187.7 7.2 fusion.405
  194.9 12.3 %slice_add_fusion.16 = (f32[32,1,1024]{2,1,0:T(1,128)S(1)}, f32[32,1,1024]{2,1,0:T(1,128)S(1)}, f32[32,1,1024]{2,1,0:T(1,128)S(1)}) fusion(f32[32,64,1087]{2,1,0:T(8,128)} %bitcast.1065), kind=kLoop, calls=%fused_computation.364 | loop fusion | flops 524288 | bytes 2883584 | tf_op jit(solution)/shard_map/add | solution.py:65
  209.4 34.8 %psum.86 = f32[32,64]{1,0:T(8,128)S(1)} all-reduce(f32[32,64]{1,0:T(8,128)S(1)} %get-tuple-element.8), channel_id=1, replica_groups=mesh['tm'=8,'neuron'=8,'motif'=2] {'neuron'}, use_global_device_ids=true, to_apply=%region_3.0 | all-reduce | flops 2048 | bytes 16384 | tf_op jit(solution)/shard_map/psum | solution.py:67
  244.2 44.5 %all-reduce.11.cloned.1.call-done = f32[32,1024]{1,0:T(8,128)} async-done(((f32[32,1024]{1,0:T(8,128)}), f32[32,1024]{1,0:T(8,128)}) %all-reduce.11.cloned.1.call-update) | async-done | bytes 131088 | tf_op jit(solution)/shard_map/psum | solution.py:67
  290.0 9.1 %collective-permute-start.2 = (bf16[32,63]{1,0:T(8,128)(2,1)S(1)}, bf16[32,63]{1,0:T(8,128)(2,1)S(1)}, u32[]{:S(2)}, u32[]{:S(2)}) collective-permute-start(bf16[32,63]{1,0:T(8,128)(2,1)S(1)} %slice.1541), channel_id=1, source_target_pairs={{0,16},{16,32},{32,48},{48,64},{64,80},{80,96},{96,112},{1,17},{17... | collective-permute-start | bytes 12104 | tf_op jit(solution)/shard_map/ppermute | solution.py:14
  310.6 6.5 copy.6240
  317.1 38.1 %all-reduce.13.cloned.1.call-done = f32[256,1024]{0,1:T(8,128)} async-done(((f32[256,1024]{0,1:T(8,128)}), f32[256,1024]{0,1:T(8,128)}) %all-reduce.13.cloned.1.call-update) | async-done | bytes 1048592 | tf_op jit(solution)/shard_map/psum | solution.py:49
  355.2 5.1 fusion.13
  360.4 2.9 convert_reduce_fusion.1
  363.5 12.8 %psum.89 = f32[2048]{0:T(1024)S(1)} all-reduce(f32[2048]{0:T(1024)S(1)} %reduce_sum.44), channel_id=1, replica_groups=mesh['tm'=8,'neuron'=8,'motif'=2] {'tm'}, use_global_device_ids=true, to_apply=%region_7.0 | all-reduce | flops 2048 | bytes 16384 | tf_op jit(solution)/shard_map/psum | solution.py:76
  376.3 49.2 %all-reduce.15.cloned.1.call-done = f32[2048,256]{1,0:T(8,128)} async-done(((f32[2048,256]{1,0:T(8,128)}), f32[2048,256]{1,0:T(8,128)}) %all-reduce.15.cloned.1.call-update) | async-done | bytes 2097168 | tf_op jit(solution)/shard_map/psum | solution.py:76
  431.6 48.2 %all-reduce.17.cloned.1.call-done = f32[256,1024]{0,1:T(8,128)} async-done(((f32[256,1024]{0,1:T(8,128)}), f32[256,1024]{0,1:T(8,128)}) %all-reduce.17.cloned.1.call-update) | async-done | bytes 1048592 | tf_op jit(solution)/shard_map/psum | solution.py:49
  489.5 6.0 fusion.400
  495.5 5.8 fusion.401
  503.5 5.6 slice_add_fusion
  511.4 34.6 %psum.92 = f32[32,64]{1,0:T(8,128)S(1)} all-reduce(f32[32,64]{1,0:T(8,128)S(1)} %reduce_sum.46), channel_id=1, replica_groups=mesh['tm'=8,'neuron'=8,'motif'=2] {'neuron'}, use_global_device_ids=true, to_apply=%region_11.0 | all-reduce | flops 2048 | bytes 16384 | tf_op jit(solution)/shard_map/psum | solution.py:67
  546.0 44.6 %all-reduce.19.cloned.1.call-done = f32[32,1024]{1,0:T(8,128)} async-done(((f32[32,1024]{1,0:T(8,128)}), f32[32,1024]{1,0:T(8,128)}) %all-reduce.19.cloned.1.call-update) | async-done | bytes 131088 | tf_op jit(solution)/shard_map/psum | solution.py:67
  592.5 9.1 %collective-permute-start.4 = (bf16[32,63]{1,0:T(8,128)(2,1)S(1)}, bf16[32,63]{1,0:T(8,128)(2,1)S(1)}, u32[]{:S(2)}, u32[]{:S(2)}) collective-permute-start(bf16[32,63]{1,0:T(8,128)(2,1)S(1)} %slice.1731), channel_id=1, source_target_pairs={{0,16},{16,32},{32,48},{48,64},{64,80},{80,96},{96,112},{1,17},{17... | collective-permute-start | bytes 12104 | tf_op jit(solution)/shard_map/ppermute | solution.py:14
  615.6 44.7 %all-reduce.21.cloned.1.call-done = f32[256,1024]{0,1:T(8,128)} async-done(((f32[256,1024]{0,1:T(8,128)}), f32[256,1024]{0,1:T(8,128)}) %all-reduce.21.cloned.1.call-update) | async-done | bytes 1048592 | tf_op jit(solution)/shard_map/psum | solution.py:49
  660.4 5.1 fusion.14
  665.5 2.8 convert_reduce_fusion
  668.4 12.8 %psum.95 = f32[2048]{0:T(1024)S(1)} all-reduce(f32[2048]{0:T(1024)S(1)} %reduce_sum.48), channel_id=1, replica_groups=mesh['tm'=8,'neuron'=8,'motif'=2] {'tm'}, use_global_device_ids=true, to_apply=%region_15.0 | all-reduce | flops 2048 | bytes 16384 | tf_op jit(solution)/shard_map/psum | solution.py:76
  681.3 49.3 %all-reduce.23.cloned.1.call-done = f32[2048,256]{1,0:T(8,128)} async-done(((f32[2048,256]{1,0:T(8,128)}), f32[2048,256]{1,0:T(8,128)}) %all-reduce.23.cloned.1.call-update) | async-done | bytes 2097168 | tf_op jit(solution)/shard_map/psum | solution.py:76
  730.6 3.5 multiply_divide_fusion
  (276 shorter events, 105.6 us)
Async XLA Ops:
  7.2 8.4 %copy-start.10 = (f32[32,1024]{1,0:T(8,128)S(1)}, f32[32,1024]{1,0:T(8,128)}, u32[]{:S(2)}) copy-start(f32[32,1024]{1,0:T(8,128)} %param.5) | copy-start | bytes 393220
  7.2 135.0 %all-reduce.9.cloned.1.call-start = ((), (), s32[]{:S(2)}) async-start(), calls=%async_computation | async-start | bytes 2097152 | tf_op jit(solution)/shard_map/psum | solution.py:49
  8.2 7.4 %collective-permute-start = (bf16[32,63]{1,0:T(8,128)(2,1)S(1)}, bf16[32,63]{1,0:T(8,128)(2,1)S(1)}, u32[]{:S(2)}, u32[]{:S(2)}) collective-permute-start(bf16[32,63]{1,0:T(8,128)(2,1)S(1)} %slice.1351), channel_id=1, source_target_pairs={{0,16},{16,32},{32,48},{48,64},{64,80},{80,96},{96,112},{1,17},{17... | collective-permute-start | bytes 12104 | tf_op jit(solution)/shard_map/ppermute | solution.py:14
  15.5 73.7 %copy-start.8 = (bf16[32,64,256]{2,1,0:T(8,128)(2,1)}, bf16[32,64,256]{2,1,0:T(8,128)(2,1)S(1)}, u32[]{:S(2)}) copy-start(bf16[32,64,256]{2,1,0:T(8,128)(2,1)S(1)} %get-tuple-element.9) | copy-start | bytes 3145732
  89.3 4.6 copy-start.7
  93.8 194.9 %all-reduce.11.cloned.1.call-start = ((), (), s32[]{:S(2)}) async-start(), calls=%async_computation.1 | async-start | bytes 262144 | tf_op jit(solution)/shard_map/psum | solution.py:67
  143.6 5.4 collective-permute-start.1
  194.9 93.9 %copy-start.11 = (f32[32,1024]{1,0:T(8,128)S(1)}, f32[32,1024]{1,0:T(8,128)}, u32[]{:S(2)}) copy-start(f32[32,1024]{1,0:T(8,128)} %param.5) | copy-start | bytes 393220
  209.4 145.8 %all-reduce.13.cloned.1.call-start = ((), (), s32[]{:S(2)}) async-start(), calls=%async_computation.2 | async-start | bytes 2097152 | tf_op jit(solution)/shard_map/psum | solution.py:49
  290.0 9.9 %collective-permute-start.2 = (bf16[32,63]{1,0:T(8,128)(2,1)S(1)}, bf16[32,63]{1,0:T(8,128)(2,1)S(1)}, u32[]{:S(2)}, u32[]{:S(2)}) collective-permute-start(bf16[32,63]{1,0:T(8,128)(2,1)S(1)} %slice.1541), channel_id=1, source_target_pairs={{0,16},{16,32},{32,48},{48,64},{64,80},{80,96},{96,112},{1,17},{17... | collective-permute-start | bytes 12104 | tf_op jit(solution)/shard_map/ppermute | solution.py:14
  300.2 7.8 %copy-start.9 = (bf16[32,64,256]{2,1,0:T(8,128)(2,1)S(1)}, bf16[32,64,256]{2,1,0:T(8,128)(2,1)}, u32[]{:S(2)}) copy-start(bf16[32,64,256]{2,1,0:T(8,128)(2,1)} %copy-done.8) | copy-start | bytes 3145732
  305.9 2.0 copy-start.2
  310.4 115.0 %all-reduce.15.cloned.1.call-start = ((), (), s32[]{:S(2)}) async-start(), calls=%async_computation.3 | async-start | bytes 4194304 | tf_op jit(solution)/shard_map/psum | solution.py:76
  360.3 65.1 %copy-start = (f32[32,64,256]{2,1,0:T(8,128)S(1)}, f32[32,64,256]{2,1,0:T(8,128)}, u32[]{:S(2)}) copy-start(f32[32,64,256]{2,1,0:T(8,128)} %param.4) | copy-start | bytes 6291460
  360.3 119.5 %all-reduce.17.cloned.1.call-start = ((), (), s32[]{:S(2)}) async-start(), calls=%async_computation.4 | async-start | bytes 2097152 | tf_op jit(solution)/shard_map/psum | solution.py:49
  425.4 3.4 copy-start.5
  427.8 1.0 copy-start.3
  431.6 159.0 %all-reduce.19.cloned.1.call-start = ((), (), s32[]{:S(2)}) async-start(), calls=%async_computation.5 | async-start | bytes 262144 | tf_op jit(solution)/shard_map/psum | solution.py:67
  481.3 5.4 collective-permute-start.3
  511.3 149.1 %all-reduce.21.cloned.1.call-start = ((), (), s32[]{:S(2)}) async-start(), calls=%async_computation.6 | async-start | bytes 2097152 | tf_op jit(solution)/shard_map/psum | solution.py:49
  592.5 9.9 %collective-permute-start.4 = (bf16[32,63]{1,0:T(8,128)(2,1)S(1)}, bf16[32,63]{1,0:T(8,128)(2,1)S(1)}, u32[]{:S(2)}, u32[]{:S(2)}) collective-permute-start(bf16[32,63]{1,0:T(8,128)(2,1)S(1)} %slice.1731), channel_id=1, source_target_pairs={{0,16},{16,32},{32,48},{48,64},{64,80},{80,96},{96,112},{1,17},{17... | collective-permute-start | bytes 12104 | tf_op jit(solution)/shard_map/ppermute | solution.py:14
  608.4 2.4 copy-start.1
  608.4 4.3 copy-start.4
  610.8 2.0 copy-start.6
  615.6 115.0 %all-reduce.23.cloned.1.call-start = ((), (), s32[]{:S(2)}) async-start(), calls=%async_computation.7 | async-start | bytes 4194304 | tf_op jit(solution)/shard_map/psum | solution.py:76
Sparse Core Ops, SparseCore 0:
  93.9 48.2 all-reduce.8
  209.5 79.1 all-reduce.10
  310.5 44.6 all-reduce.12
  360.5 64.9 all-reduce.14
  431.7 48.1 all-reduce.16
  511.4 79.1 all-reduce.18
  615.7 44.6 all-reduce.20
  665.6 64.9 all-reduce.22
where the time goes:
time: 752 us; the launch traced here: 741 us
  waiting for transfers between devices  374 us (50%)
  local copies, waits for them, and re-layouts  141 us (19%)
  blocking collectives  95 us (13%)
  other arithmetic  53.6 us (7%)
  matrix products  33.3 us (4%)
  starting transfers between devices  28.8 us (4%)
  between operations  15.9 us (2%)
    psum x4, waiting for transfers between devices, ratio_and_lagged(): estimated_counts = lax.psum(part, 'motif')  179 us
    psum x2, waiting for transfers between devices, local(): wnum, wden = lax.psum((wnum, wden), 'tm')  98.5 us
    psum x2, waiting for transfers between devices, local(): hnum, colsum = lax.psum((hnum, colsum), 'neuron')  89.1 us
    another operation x67, local copies, waits for them, and re-layouts, stacked(): return jnp.stack(rows, axis=1).reshape(count * (rim + 1), width)  80.3 us
    psum x2, blocking collectives, local(): hnum, colsum = lax.psum((hnum, colsum), 'neuron')  69.4 us
    slice x6, local copies, waits for them, and re-layouts, local(): hnum = hnum + prod[:, lag, lag:lag + width]  45.2 us
    ppermute x5, starting transfers between devices, from_behind(): lax.ppermute(value, axis, [(source, source + steps) for source in range(f...  28.3 us
    psum x2, blocking collectives, local(): wnum, wden = lax.psum((wnum, wden), 'tm')  25.6 us
  transfers between devices with their start and end apart: 13, of which 12 were waited for; matrix products, arithmetic and copies ran while one was open for 2% of the time, Pallas kernels for 0%

commit v1 on v0

--- a/solution.py
+++ b/solution.py
@@ -14,6 +14,61 @@
     return lax.ppermute(value, axis, [(source, source + steps) for source in range(first, last)])
 
 
+def xor_swap(value, axis, mask):
+    count = lax.axis_size(axis)
+    return lax.ppermute(value, axis, [(source, source ^ mask) for source in range(count)])
+
+
+def masks_of(axis):
+    count = lax.axis_size(axis)
+    masks = []
+    mask = 1
+    while mask < count:
+        masks.append(mask)
+        mask *= 2
+    return masks
+
+
+def all_sum(value, axis):
+    for mask in masks_of(axis):
+        value = jax.tree.map(lambda a, b: a + b, value, xor_swap(value, axis, mask))
+    return value
+
+
+def bit_of(axis, mask):
+    return (lax.axis_index(axis) // mask) % 2 == 1
+
+
+def sum_scatter(value, axis):
+    for mask in masks_of(axis):
+        half = value.shape[0] // 2
+        low, high = value[:half], value[half:]
+        upper = bit_of(axis, mask)
+        send = jnp.where(upper, low, high)
+        keep = jnp.where(upper, high, low)
+        value = keep + xor_swap(send, axis, mask)
+    return value
+
+
+def scatter_offset(axis, rows):
+    offset = 0
+    size = rows
+    for mask in masks_of(axis):
+        size //= 2
+        offset = offset + jnp.where(bit_of(axis, mask), size, 0)
+    return offset
+
+
+def gather_rows(value, axis):
+    for mask in reversed(masks_of(axis)):
+        other = xor_swap(value, axis, mask)
+        upper = bit_of(axis, mask)
+        value = jnp.where(
+            upper, jnp.concatenate([other, value], axis=0), jnp.concatenate([value, other], axis=0)
+        )
+    return value
+
+
 def stacked(hext, count, rim, width):
     rows = [hext[:, rim - lag : rim - lag + width] for lag in range(rim + 1)]
     return jnp.stack(rows, axis=1).reshape(count * (rim + 1), width)
@@ -23,15 +78,19 @@
     k_dev, lags, n_dev = motif_w.shape
     width = counts.shape[1]
     rim = lags - 1
+    rows = k_dev * lags
     scale_factor = 1.0 / (MOTIFS * LAGS)
     total_bins = width * lax.axis_size("tm")
     leading_bin = lax.axis_index("tm") * width
     reduce_over_rows = (((0,), (0,)), ((), ()))
     contract_cols = (((1,), (1,)), ((), ()))
     spike_events = counts.astype(jnp.float32)
-    weights = motif_w.reshape(k_dev * lags, n_dev)
+    weights = motif_w.reshape(rows, n_dev)
     weight_bfloat = weights.astype(jnp.bfloat16)
     acts = motif_h
+    offset = scatter_offset("tm", rows)
+    part_rows = rows // lax.axis_size("tm")
+    weight_part = lax.dynamic_slice_in_dim(weights, offset, part_rows, axis=0)
 
     def extend_padded(acts):
         hbf = acts.astype(jnp.bfloat16)
@@ -46,7 +105,7 @@
             )
             * scale_factor
         )
-        estimated_counts = lax.psum(part, "motif")
+        estimated_counts = part + xor_swap(part, "motif", 1)
         return ((spike_events / estimated_counts).astype(jnp.bfloat16), lagged_copies)
 
     bins = leading_bin + jnp.arange(width, dtype=jnp.int32)
@@ -64,7 +123,7 @@
         for lag in range(lags):
             hnum = hnum + prod[:, lag, lag : lag + width]
         colsum = jnp.sum(weight_bfloat.reshape(k_dev, lags, n_dev), axis=2, dtype=jnp.float32)
-        hnum, colsum = lax.psum((hnum, colsum), "neuron")
+        hnum, colsum = all_sum((hnum, colsum), "neuron")
         hden = jnp.dot(colsum, mask, precision=lax.Precision.HIGHEST)
         acts = acts * hnum / hden
         hext = extend_padded(acts)
@@ -73,9 +132,13 @@
             lagged_copies, ratio, contract_cols, preferred_element_type=jnp.float32
         )
         wden = jnp.sum(lagged_copies, axis=1, dtype=jnp.float32)
-        wnum, wden = lax.psum((wnum, wden), "tm")
-        weights = weights * wnum / wden[:, None]
-        weight_bfloat = weights.astype(jnp.bfloat16)
+        wnum = sum_scatter(wnum, "tm")
+        wden = all_sum(wden, "tm")
+        wden_part = lax.dynamic_slice_in_dim(wden, offset, part_rows, axis=0)
+        weight_part = weight_part * wnum / wden_part[:, None]
+        if step + 1 < ITERS:
+            weight_bfloat = gather_rows(weight_part.astype(jnp.bfloat16), "tm")
+    weights = gather_rows(weight_part, "tm")
     return (weights.reshape(k_dev, lags, n_dev), acts)
 
 

time: 752 us -> 495 us (0.66)
  waiting for transfers between devices: 374 us -> 183 us
  blocking collectives: 95 us -> 0 us
  starting transfers between devices: 28.8 us -> 86.4 us
  between operations: 15.9 us -> 2.39 us
  local copies, waits for them, and re-layouts: 141 us -> 132 us
    psum x8 -> x0, waiting for transfers between devices: 367 us -> none  [the longest x4 179 us: ratio_and_lagged(): estimated_counts = lax.psum(part, 'motif')]
    ppermute x0 -> x34, waiting for transfers between devices: none -> 176 us  [xor_swap(): lax.ppermute(value, axis, [(source, source ^ mask) for source in range(co...]
    psum x4 -> x0, blocking collectives: 95 us -> none  [the longest x2 69.4 us: local(): hnum, colsum = lax.psum((hnum, colsum), 'neuron')]
    ppermute x0 -> x34, starting transfers between devices: none -> 60.9 us  [xor_swap(): lax.ppermute(value, axis, [(source, source ^ mask) for source in range(co...]
    another operation x67, local copies, waits for them, and re-layouts: 80.3 us -> 71.8 us  [stacked(): return jnp.stack(rows, axis=1).reshape(count * (rim + 1), width)]
  transfers between devices with their start and end apart: 13 -> 39, of which waited for: 12 -> 34; matrix products, arithmetic and copies ran while one was open for 2% -> 3% of each run, Pallas kernels for 0% -> 0%
where the time goes in v1:
time: 495 us; the launch traced here: 485 us
  waiting for transfers between devices  183 us (37%)
  local copies, waits for them, and re-layouts  132 us (27%)
  starting transfers between devices  86.4 us (17%)
  other arithmetic  55.5 us (11%)
  matrix products  27 us (5%)
    ppermute x34, waiting for transfers between devices, xor_swap(): lax.ppermute(value, axis, [(source, source ^ mask) for source in range(co...  176 us
    another operation x67, local copies, waits for them, and re-layouts, stacked(): return jnp.stack(rows, axis=1).reshape(count * (rim + 1), width)  71.8 us
    ppermute x34, starting transfers between devices, xor_swap(): lax.ppermute(value, axis, [(source, source ^ mask) for source in range(co...  60.9 us
    slice x6, local copies, waits for them, and re-layouts, local(): hnum = hnum + prod[:, lag, lag:lag + width]  44.8 us
    ppermute x5, starting transfers between devices, from_behind(): lax.ppermute(value, axis, [(source, source + steps) for source in range(f...  25.4 us
    add x4, other arithmetic, local(): hnum = hnum + prod[:, lag, lag:lag + width]  22.8 us
    dot_general x4, matrix products, ratio_and_lagged(): lax.dot_general(weight_bfloat, lagged_copies, reduce_over_rows, preferred...  12.7 us
    unnamed x124, other arithmetic  11.2 us
  transfers between devices with their start and end apart: 39, of which 34 were waited for; matrix products, arithmetic and copies ran while one was open for 3% of the time, Pallas kernels for 0%

profile of v1, /device:TPU:1, one launch (start us, length us, event | category | flops | bytes accessed | tf_op | source)
XLA Modules:
  0.0 485.4 jit_solution(14324717493576176700)
XLA Ops:
  1.6 4.6 collective-permute-start
  47.9 28.5 %stack.714 = bf16[32,64,1024]{2,1,0:T(8,128)(2,1)} concatenate(bf16[32,1,1024]{2,1,0:T(2,128)(2,1)S(1)} %copy.6179, bf16[32,1,1024]{2,1,0:T(2,128)(2,1)S(1)} %copy.6180, bf16[32,1,1024]{2,1,0:T(2,128)(2,1)S(1)} %copy.6181, bf16[32,1,1024]{2,1,0:T(2,128)(2,1)S(1)} %copy.6182, bf16[32,1,1024]{2,1,0:T(2,128)(2,1)S(1)} %copy.6183, bf16[32,1,1024]{2,1,0:T(2,128)(2,1)S(1)} %copy.6184, ...), dimensions={1} | concatenate | bytes 8388608 | tf_op jit(solution)/shard_map/stack | solution.py:74
  76.4 4.4 fusion.1
  84.0 21.0 %collective-permute-done.1 = f32[256,1024]{0,1:T(8,128)} collective-permute-done((f32[256,1024]{0,1:T(8,128)}, f32[256,1024]{0,1:T(8,128)}, u32[]{:S(2)}, u32[]{:S(2)}) %collective-permute-start.1) | collective-permute-done | bytes 1048608 | tf_op jit(solution)/shard_map/ppermute | solution.py:19
  112.1 4.8 convolution_bitcast_fusion
  116.9 9.7 %copy.6243 = f32[2048,1087]{1,0:T(8,128)} copy(f32[2048,1087]{0,1:T(8,128)} %convolution_bitcast_fusion) | data formatting | bytes 17809408 | tf_op jit(solution)/shard_map/dot_general | solution.py:119
  126.6 11.6 %fusion.408 = (f32[32,1,1024]{2,1,0:T(1,128)S(1)}, f32[32,1,1024]{2,1,0:T(1,128)S(1)}, f32[32,1,1024]{2,1,0:T(1,128)S(1)}, f32[32,1,1024]{2,1,0:T(1,128)S(1)}, f...) fusion(f32[32,64,1087]{2,1,0:T(8,128)} %bitcast.1047), kind=kLoop, calls=%fused_computation.886 | loop fusion | bytes 4980736 | tf_op jit(solution)/shard_map/slice | solution.py:124
  138.2 12.1 %fusion.409 = (f32[32,1,1024]{2,1,0:T(1,128)S(1)}, f32[32,1,1024]{2,1,0:T(1,128)S(1)}, f32[32,1,1024]{2,1,0:T(1,128)S(1)}, f32[32,1,1024]{2,1,0:T(1,128)S(1)}, f...) fusion(f32[32,64,1087]{2,1,0:T(8,128)} %bitcast.1048), kind=kLoop, calls=%fused_computation.887 | loop fusion | bytes 4980736 | tf_op jit(solution)/shard_map/slice | solution.py:124
  150.3 7.2 %fusion.410 = (f32[32,1,1024]{2,1,0:T(1,128)S(1)}, f32[32,1,1024]{2,1,0:T(1,128)S(1)}, f32[32,1,1024]{2,1,0:T(1,128)S(1)}, f32[32,1,1024]{2,1,0:T(1,128)S(1)}, f...) fusion(f32[32,64,1087]{2,1,0:T(8,128)} %bitcast.1049), kind=kLoop, calls=%fused_computation.888 | loop fusion | bytes 1835008 | tf_op jit(solution)/shard_map/slice | solution.py:124
  157.6 12.6 %slice_add_fusion.16 = (f32[32,1,1024]{2,1,0:T(1,128)S(1)}, f32[32,1,1024]{2,1,0:T(1,128)S(1)}, f32[32,1,1024]{2,1,0:T(1,128)S(1)}) fusion(f32[32,64,1087]{2,1,0:T(8,128)} %bitcast.1050), kind=kLoop, calls=%fused_computation.379 | loop fusion | flops 524288 | bytes 2883584 | tf_op jit(solution)/shard_map/add | solution.py:124
  172.7 3.8 collective-permute-start.3
  199.1 8.4 %collective-permute-start.9 = (bf16[32,63]{1,0:T(8,128)(2,1)S(1)}, bf16[32,63]{1,0:T(8,128)(2,1)S(1)}, u32[]{:S(2)}, u32[]{:S(2)}) collective-permute-start(bf16[32,63]{1,0:T(8,128)(2,1)S(1)} %slice.1589), channel_id=1, source_target_pairs={{0,16},{16,32},{32,48},{48,64},{64,80},{80,96},{96,112},{1,17},{17... | collective-permute-start | bytes 12104 | tf_op jit(solution)/shard_map/ppermute | solution.py:14
  218.6 4.5 copy.6244
  223.1 16.4 %collective-permute-done.10 = f32[256,1024]{0,1:T(8,128)} collective-permute-done((f32[256,1024]{0,1:T(8,128)}, f32[256,1024]{0,1:T(8,128)}, u32[]{:S(2)}, u32[]{:S(2)}) %collective-permute-start.10) | collective-permute-done | bytes 1048608 | tf_op jit(solution)/shard_map/ppermute | solution.py:19
  251.7 4.8 collective-permute-start.12
  256.5 12.2 %collective-permute-done.12 = f32[512,256]{1,0:T(8,128)} collective-permute-done((f32[512,256]{1,0:T(8,128)}, f32[512,256]{1,0:T(8,128)}, u32[]{:S(2)}, u32[]{:S(2)}) %collective-permute-start.12) | collective-permute-done | bytes 524320 | tf_op jit(solution)/shard_map/ppermute | solution.py:19
  288.1 3.9 collective-permute-done.17
  292.7 4.7 collective-permute-done.18
  297.6 5.0 %collective-permute-start.19 = (bf16[1024,256]{1,0:T(8,128)(2,1)S(1)}, bf16[1024,256]{1,0:T(8,128)(2,1)S(1)}, u32[]{:S(2)}, u32[]{:S(2)}) collective-permute-start(bf16[1024,256]{1,0:T(8,128)(2,1)S(1)} %maximum_select_fusion.3), channel_id=1, source_target_pairs={{0,16},{16,0},{32,48},{48,32},{64,80},{80,64},{96,112},{112,96},{1... | collective-permute-start | bytes 1572872 | tf_op jit(solution)/shard_map/ppermute | solution.py:19
  304.2 3.9 convolution_multiply_fusion.1
  309.5 23.1 %collective-permute-done.20 = f32[256,1024]{0,1:T(8,128)S(1)} collective-permute-done((f32[256,1024]{0,1:T(8,128)S(1)}, f32[256,1024]{0,1:T(8,128)S(1)}, u32[]{:S(2)}, u32[]{:S(2)}) %collective-permute-start.20) | collective-permute-done | bytes 1048608 | tf_op jit(solution)/shard_map/ppermute | solution.py:19
  339.6 6.0 %fusion.405 = (f32[32,1,1024]{2,1,0:T(1,128)S(1)}, f32[32,1,1024]{2,1,0:T(1,128)S(1)}, f32[32,1,1024]{2,1,0:T(1,128)S(1)}, f32[32,1,1024]{2,1,0:T(1,128)S(1)}, f...) fusion(f32[32,64,1087]{2,1,0:T(8,128)S(1)} %bitcast.1043), kind=kLoop, calls=%fused_computation.883 | loop fusion | bytes 4980736 | tf_op jit(solution)/shard_map/slice | solution.py:124
  345.6 5.8 %fusion.406 = (f32[32,1,1024]{2,1,0:T(1,128)S(1)}, f32[32,1,1024]{2,1,0:T(1,128)S(1)}, f32[32,1,1024]{2,1,0:T(1,128)S(1)}, f32[32,1,1024]{2,1,0:T(1,128)S(1)}, f...) fusion(f32[32,64,1087]{2,1,0:T(8,128)S(1)} %bitcast.1044), kind=kLoop, calls=%fused_computation.884 | loop fusion | bytes 4980736 | tf_op jit(solution)/shard_map/slice | solution.py:124
  353.5 5.3 %slice_add_fusion = (f32[32,1,1024]{2,1,0:T(1,128)S(1)}, f32[32,1,1024]{2,1,0:T(1,128)S(1)}, f32[32,1,1024]{2,1,0:T(1,128)S(1)}) fusion(f32[32,64,1087]{2,1,0:T(8,128)S(1)} %bitcast.1046), kind=kLoop, calls=%fused_computation.363 | loop fusion | flops 524288 | bytes 2883584 | tf_op jit(solution)/shard_map/add | solution.py:124
  361.3 3.3 collective-permute-start.22
  367.8 5.1 %collective-permute-done.23 = f32[32,1024]{1,0:T(8,128)S(1)} collective-permute-done((f32[32,1024]{1,0:T(8,128)S(1)}, f32[32,1024]{1,0:T(8,128)S(1)}, u32[]{:S(2)}, u32[]{:S(2)}) %collective-permute-start.23) | collective-permute-done | bytes 131104 | tf_op jit(solution)/shard_map/ppermute | solution.py:19
  386.3 7.4 %collective-permute-start.28 = (bf16[32,63]{1,0:T(8,128)(2,1)S(1)}, bf16[32,63]{1,0:T(8,128)(2,1)S(1)}, u32[]{:S(2)}, u32[]{:S(2)}) collective-permute-start(bf16[32,63]{1,0:T(8,128)(2,1)S(1)} %slice.1785), channel_id=1, source_target_pairs={{0,16},{16,32},{32,48},{48,64},{64,80},{80,96},{96,112},{1,17},{17... | collective-permute-start | bytes 12104 | tf_op jit(solution)/shard_map/ppermute | solution.py:14
  406.1 22.4 %collective-permute-done.29 = f32[256,1024]{0,1:T(8,128)S(1)} collective-permute-done((f32[256,1024]{0,1:T(8,128)S(1)}, f32[256,1024]{0,1:T(8,128)S(1)}, u32[]{:S(2)}, u32[]{:S(2)}) %collective-permute-start.29) | collective-permute-done | bytes 1048608 | tf_op jit(solution)/shard_map/ppermute | solution.py:19
  434.7 11.9 %collective-permute-done.31 = f32[512,256]{1,0:T(8,128)S(1)} collective-permute-done((f32[512,256]{1,0:T(8,128)S(1)}, f32[512,256]{1,0:T(8,128)S(1)}, u32[]{:S(2)}, u32[]{:S(2)}) %collective-permute-start.31) | collective-permute-done | bytes 524320 | tf_op jit(solution)/shard_map/ppermute | solution.py:19
  461.5 5.2 %collective-permute-done.36 = f32[256,256]{1,0:T(8,128)S(1)} collective-permute-done((f32[256,256]{1,0:T(8,128)S(1)}, f32[256,256]{1,0:T(8,128)S(1)}, u32[]{:S(2)}, u32[]{:S(2)}) %collective-permute-start.36) | collective-permute-done | bytes 262176 | tf_op jit(solution)/shard_map/ppermute | solution.py:19
  467.2 9.3 %collective-permute-done.37 = f32[512,256]{1,0:T(8,128)S(1)} collective-permute-done((f32[512,256]{1,0:T(8,128)S(1)}, f32[512,256]{1,0:T(8,128)S(1)}, u32[]{:S(2)}, u32[]{:S(2)}) %collective-permute-start.37) | collective-permute-done | bytes 524320 | tf_op jit(solution)/shard_map/ppermute | solution.py:19
  476.6 4.7 collective-permute-start.38
  (340 shorter events, 189.3 us)
Async XLA Ops:
  1.6 7.7 %collective-permute-start = (bf16[32,63]{1,0:T(8,128)(2,1)S(1)}, bf16[32,63]{1,0:T(8,128)(2,1)S(1)}, u32[]{:S(2)}, u32[]{:S(2)}) collective-permute-start(bf16[32,63]{1,0:T(8,128)(2,1)S(1)} %slice.1399), channel_id=1, source_target_pairs={{0,16},{16,32},{32,48},{48,64},{64,80},{80,96},{96,112},{1,17},{17... | collective-permute-start | bytes 12104 | tf_op jit(solution)/shard_map/ppermute | solution.py:14
  80.8 24.2 %collective-permute-start.1 = (f32[256,1024]{0,1:T(8,128)}, f32[256,1024]{0,1:T(8,128)}, u32[]{:S(2)}, u32[]{:S(2)}) collective-permute-start(f32[256,1024]{0,1:T(8,128)} %fusion.1), channel_id=1, source_target_pairs={{0,1},{1,0},{2,3},{3,2},{4,5},{5,4},{6,7},{7,6},{8,9},{9,8},{10,11... | collective-permute-start | bytes 3145736 | tf_op jit(solution)/shard_map/ppermute | solution.py:19
  106.8 5.2 %collective-permute-start.2 = (bf16[256,63]{0,1:T(8,128)(2,1)S(1)}, bf16[256,63]{0,1:T(8,128)(2,1)S(1)}, u32[]{:S(2)}, u32[]{:S(2)}) collective-permute-start(bf16[256,63]{0,1:T(8,128)(2,1)S(1)} %slice.1524), channel_id=1, source_target_pairs={{16,0},{32,16},{48,32},{64,48},{80,64},{96,80},{112,96},{17,1},{33... | collective-permute-start | bytes 96776 | tf_op jit(solution)/shard_map/ppermute | solution.py:14
  172.7 6.1 %collective-permute-start.3 = (f32[32,1024]{1,0:T(8,128)S(1)}, f32[32,1024]{1,0:T(8,128)S(1)}, u32[]{:S(2)}, u32[]{:S(2)}) collective-permute-start(f32[32,1024]{1,0:T(8,128)S(1)} %bitcast_add_fusion.47), channel_id=1, source_target_pairs={{0,2},{2,0},{4,6},{6,4},{8,10},{10,8},{12,14},{14,12},{1,3},{3,1},... | collective-permute-start | bytes 393224 | tf_op jit(solution)/shard_map/ppermute | solution.py:19
  178.8 4.5 collective-permute-start.4
  183.3 13.9 %collective-permute-start.5 = (f32[32,1024]{1,0:T(8,128)S(1)}, f32[32,1024]{1,0:T(8,128)}, u32[]{:S(2)}, u32[]{:S(2)}) collective-permute-start(f32[32,1024]{1,0:T(8,128)S(1)} %add.605), channel_id=1, source_target_pairs={{0,8},{2,10},{4,12},{6,14},{8,0},{10,2},{12,4},{14,6},{1,9},{3,11}... | collective-permute-start | bytes 393224 | tf_op jit(solution)/shard_map/ppermute | solution.py:19
  186.2 4.4 collective-permute-start.6
  193.2 4.1 collective-permute-start.8
  199.1 9.2 %collective-permute-start.9 = (bf16[32,63]{1,0:T(8,128)(2,1)S(1)}, bf16[32,63]{1,0:T(8,128)(2,1)S(1)}, u32[]{:S(2)}, u32[]{:S(2)}) collective-permute-start(bf16[32,63]{1,0:T(8,128)(2,1)S(1)} %slice.1589), channel_id=1, source_target_pairs={{0,16},{16,32},{32,48},{48,64},{64,80},{80,96},{96,112},{1,17},{17... | collective-permute-start | bytes 12104 | tf_op jit(solution)/shard_map/ppermute | solution.py:14
  216.9 22.6 %collective-permute-start.10 = (f32[256,1024]{0,1:T(8,128)}, f32[256,1024]{0,1:T(8,128)}, u32[]{:S(2)}, u32[]{:S(2)}) collective-permute-start(f32[256,1024]{0,1:T(8,128)} %fusion.3), channel_id=1, source_target_pairs={{0,1},{1,0},{2,3},{3,2},{4,5},{5,4},{6,7},{7,6},{8,9},{9,8},{10,11... | collective-permute-start | bytes 3145736 | tf_op jit(solution)/shard_map/ppermute | solution.py:19
  244.8 3.0 collective-permute-start.11
  251.7 17.1 %collective-permute-start.12 = (f32[512,256]{1,0:T(8,128)}, f32[512,256]{1,0:T(8,128)}, u32[]{:S(2)}, u32[]{:S(2)}) collective-permute-start(f32[512,256]{1,0:T(8,128)} %slice_select_fusion.3), channel_id=1, source_target_pairs={{0,32},{16,48},{32,0},{48,16},{64,96},{80,112},{96,64},{112,80},{1... | collective-permute-start | bytes 1572872 | tf_op jit(solution)/shard_map/ppermute | solution.py:19
  271.1 14.3 %collective-permute-start.13 = (f32[256,256]{1,0:T(8,128)S(1)}, f32[256,256]{1,0:T(8,128)}, u32[]{:S(2)}, u32[]{:S(2)}) collective-permute-start(f32[256,256]{1,0:T(8,128)S(1)} %slice_select_fusion.5), channel_id=1, source_target_pairs={{0,64},{16,80},{32,96},{48,112},{64,0},{80,16},{96,32},{112,48},{1... | collective-permute-start | bytes 786440 | tf_op jit(solution)/shard_map/ppermute | solution.py:19
  281.3 4.0 collective-permute-start.16
  286.6 5.4 %collective-permute-start.17 = (bf16[256,256]{1,0:T(8,128)(2,1)S(1)}, bf16[256,256]{1,0:T(8,128)(2,1)S(1)}, u32[]{:S(2)}, u32[]{:S(2)}) collective-permute-start(bf16[256,256]{1,0:T(8,128)(2,1)S(1)} %get-tuple-element.4), channel_id=1, source_target_pairs={{0,64},{16,80},{32,96},{48,112},{64,0},{80,16},{96,32},{112,48},{1... | collective-permute-start | bytes 393224 | tf_op jit(solution)/shard_map/ppermute | solution.py:19
  292.1 5.3 %collective-permute-start.18 = (bf16[512,256]{1,0:T(8,128)(2,1)S(1)}, bf16[512,256]{1,0:T(8,128)(2,1)S(1)}, u32[]{:S(2)}, u32[]{:S(2)}) collective-permute-start(bf16[512,256]{1,0:T(8,128)(2,1)S(1)} %maximum_select_fusion.5), channel_id=1, source_target_pairs={{0,32},{16,48},{32,0},{48,16},{64,96},{80,112},{96,64},{112,80},{1... | collective-permute-start | bytes 786440 | tf_op jit(solution)/shard_map/ppermute | solution.py:19
  297.6 6.6 %collective-permute-start.19 = (bf16[1024,256]{1,0:T(8,128)(2,1)S(1)}, bf16[1024,256]{1,0:T(8,128)(2,1)S(1)}, u32[]{:S(2)}, u32[]{:S(2)}) collective-permute-start(bf16[1024,256]{1,0:T(8,128)(2,1)S(1)} %maximum_select_fusion.3), channel_id=1, source_target_pairs={{0,16},{16,0},{32,48},{48,32},{64,80},{80,64},{96,112},{112,96},{1... | collective-permute-start | bytes 1572872 | tf_op jit(solution)/shard_map/ppermute | solution.py:19
  308.1 24.4 %collective-permute-start.20 = (f32[256,1024]{0,1:T(8,128)S(1)}, f32[256,1024]{0,1:T(8,128)S(1)}, u32[]{:S(2)}, u32[]{:S(2)}) collective-permute-start(f32[256,1024]{0,1:T(8,128)S(1)} %convolution_multiply_fusion.1), channel_id=1, source_target_pairs={{0,1},{1,0},{2,3},{3,2},{4,5},{5,4},{6,7},{7,6},{8,9},{9,8},{10,11... | collective-permute-start | bytes 3145736 | tf_op jit(solution)/shard_map/ppermute | solution.py:19
  332.8 5.2 %collective-permute-start.21 = (bf16[256,63]{0,1:T(8,128)(2,1)S(1)}, bf16[256,63]{0,1:T(8,128)(2,1)S(1)}, u32[]{:S(2)}, u32[]{:S(2)}) collective-permute-start(bf16[256,63]{0,1:T(8,128)(2,1)S(1)} %slice.1720), channel_id=1, source_target_pairs={{16,0},{32,16},{48,32},{64,48},{80,64},{96,80},{112,96},{17,1},{33... | collective-permute-start | bytes 96776 | tf_op jit(solution)/shard_map/ppermute | solution.py:14
  361.3 6.4 %collective-permute-start.22 = (f32[32,1024]{1,0:T(8,128)S(1)}, f32[32,1024]{1,0:T(8,128)S(1)}, u32[]{:S(2)}, u32[]{:S(2)}) collective-permute-start(f32[32,1024]{1,0:T(8,128)S(1)} %bitcast_add_fusion), channel_id=1, source_target_pairs={{0,2},{2,0},{4,6},{6,4},{8,10},{10,8},{12,14},{14,12},{1,3},{3,1},... | collective-permute-start | bytes 393224 | tf_op jit(solution)/shard_map/ppermute | solution.py:19
  367.7 5.2 %collective-permute-start.23 = (f32[32,1024]{1,0:T(8,128)S(1)}, f32[32,1024]{1,0:T(8,128)S(1)}, u32[]{:S(2)}, u32[]{:S(2)}) collective-permute-start(f32[32,1024]{1,0:T(8,128)S(1)} %add.687), channel_id=1, source_target_pairs={{0,4},{2,6},{4,0},{6,2},{8,12},{10,14},{12,8},{14,10},{1,5},{3,7},... | collective-permute-start | bytes 393224 | tf_op jit(solution)/shard_map/ppermute | solution.py:19
  372.9 11.5 %collective-permute-start.24 = (f32[32,1024]{1,0:T(8,128)S(1)}, f32[32,1024]{1,0:T(8,128)S(1)}, u32[]{:S(2)}, u32[]{:S(2)}) collective-permute-start(f32[32,1024]{1,0:T(8,128)S(1)} %add.688), channel_id=1, source_target_pairs={{0,8},{2,10},{4,12},{6,14},{8,0},{10,2},{12,4},{14,6},{1,9},{3,11}... | collective-permute-start | bytes 393224 | tf_op jit(solution)/shard_map/ppermute | solution.py:19
  373.6 4.1 collective-permute-start.25
  380.4 4.1 collective-permute-start.27
  386.3 8.2 %collective-permute-start.28 = (bf16[32,63]{1,0:T(8,128)(2,1)S(1)}, bf16[32,63]{1,0:T(8,128)(2,1)S(1)}, u32[]{:S(2)}, u32[]{:S(2)}) collective-permute-start(bf16[32,63]{1,0:T(8,128)(2,1)S(1)} %slice.1785), channel_id=1, source_target_pairs={{0,16},{16,32},{32,48},{48,64},{64,80},{80,96},{96,112},{1,17},{17... | collective-permute-start | bytes 12104 | tf_op jit(solution)/shard_map/ppermute | solution.py:14
  404.8 23.7 %collective-permute-start.29 = (f32[256,1024]{0,1:T(8,128)S(1)}, f32[256,1024]{0,1:T(8,128)S(1)}, u32[]{:S(2)}, u32[]{:S(2)}) collective-permute-start(f32[256,1024]{0,1:T(8,128)S(1)} %convolution_multiply_fusion), channel_id=1, source_target_pairs={{0,1},{1,0},{2,3},{3,2},{4,5},{5,4},{6,7},{7,6},{8,9},{9,8},{10,11... | collective-permute-start | bytes 3145736 | tf_op jit(solution)/shard_map/ppermute | solution.py:19
  433.0 13.6 %collective-permute-start.31 = (f32[512,256]{1,0:T(8,128)S(1)}, f32[512,256]{1,0:T(8,128)S(1)}, u32[]{:S(2)}, u32[]{:S(2)}) collective-permute-start(f32[512,256]{1,0:T(8,128)S(1)} %slice_select_fusion.2), channel_id=1, source_target_pairs={{0,32},{16,48},{32,0},{48,16},{64,96},{80,112},{96,64},{112,80},{1... | collective-permute-start | bytes 1572872 | tf_op jit(solution)/shard_map/ppermute | solution.py:19
  446.7 12.6 %collective-permute-start.32 = (f32[256,256]{1,0:T(8,128)S(1)}, f32[256,256]{1,0:T(8,128)S(1)}, u32[]{:S(2)}, u32[]{:S(2)}) collective-permute-start(f32[256,256]{1,0:T(8,128)S(1)} %slice_select_fusion.4), channel_id=1, source_target_pairs={{0,64},{16,80},{32,96},{48,112},{64,0},{80,16},{96,32},{112,48},{1... | collective-permute-start | bytes 786440 | tf_op jit(solution)/shard_map/ppermute | solution.py:19
  455.3 4.0 collective-permute-start.35
  459.5 7.2 %collective-permute-start.36 = (f32[256,256]{1,0:T(8,128)S(1)}, f32[256,256]{1,0:T(8,128)S(1)}, u32[]{:S(2)}, u32[]{:S(2)}) collective-permute-start(f32[256,256]{1,0:T(8,128)S(1)} %multiply_divide_fusion), channel_id=1, source_target_pairs={{0,64},{16,80},{32,96},{48,112},{64,0},{80,16},{96,32},{112,48},{1... | collective-permute-start | bytes 786440 | tf_op jit(solution)/shard_map/ppermute | solution.py:19
  466.7 9.8 %collective-permute-start.37 = (f32[512,256]{1,0:T(8,128)S(1)}, f32[512,256]{1,0:T(8,128)S(1)}, u32[]{:S(2)}, u32[]{:S(2)}) collective-permute-start(f32[512,256]{1,0:T(8,128)S(1)} %maximum_select_fusion.4), channel_id=1, source_target_pairs={{0,32},{16,48},{32,0},{48,16},{64,96},{80,112},{96,64},{112,80},{1... | collective-permute-start | bytes 1572872 | tf_op jit(solution)/shard_map/ppermute | solution.py:19
  476.6 7.0 %collective-permute-start.38 = (f32[1024,256]{1,0:T(8,128)S(1)}, f32[1024,256]{1,0:T(8,128)S(1)}, u32[]{:S(2)}, u32[]{:S(2)}) collective-permute-start(f32[1024,256]{1,0:T(8,128)S(1)} %maximum_select_fusion.2), channel_id=1, source_target_pairs={{0,16},{16,0},{32,48},{48,32},{64,80},{80,64},{96,112},{112,96},{1... | collective-permute-start | bytes 3145736 | tf_op jit(solution)/shard_map/ppermute | solution.py:19
  (16 other events, 175.3 us)

commit v2 on v1

--- a/solution.py
+++ b/solution.py
@@ -69,9 +69,33 @@
     return value
 
 
-def stacked(hext, count, rim, width):
-    rows = [hext[:, rim - lag : rim - lag + width] for lag in range(rim + 1)]
-    return jnp.stack(rows, axis=1).reshape(count * (rim + 1), width)
+CONV_DIMS = lax.ConvDimensionNumbers
+
+
+def recon_of(weight_bfloat, hext):
+    flipped = jnp.flip(weight_bfloat, axis=1)
+    dims = CONV_DIMS((0, 1, 2), (2, 0, 1), (0, 1, 2))
+    return lax.conv_general_dilated(
+        hext[None], flipped, (1,), [(0, 0)], dimension_numbers=dims,
+        preferred_element_type=jnp.float32,
+    )[0]
+
+
+def hnum_of(weight_bfloat, rext):
+    dims = CONV_DIMS((0, 1, 2), (0, 2, 1), (0, 1, 2))
+    return lax.conv_general_dilated(
+        rext[None], weight_bfloat, (1,), [(0, 0)], dimension_numbers=dims,
+        preferred_element_type=jnp.float32,
+    )[0]
+
+
+def wnum_of(hext, ratio):
+    dims = CONV_DIMS((1, 0, 2), (1, 0, 2), (0, 2, 1))
+    out = lax.conv_general_dilated(
+        hext[None], ratio[None], (1,), [(0, 0)], dimension_numbers=dims,
+        preferred_element_type=jnp.float32,
+    )
+    return jnp.flip(out, axis=1)
 
 
 def local(counts, motif_w, motif_h):
@@ -82,62 +106,52 @@
     scale_factor = 1.0 / (MOTIFS * LAGS)
     total_bins = width * lax.axis_size("tm")
     leading_bin = lax.axis_index("tm") * width
-    reduce_over_rows = (((0,), (0,)), ((), ()))
-    contract_cols = (((1,), (1,)), ((), ()))
     spike_events = counts.astype(jnp.float32)
     weights = motif_w.reshape(rows, n_dev)
-    weight_bfloat = weights.astype(jnp.bfloat16)
+    weight_bfloat = motif_w.astype(jnp.bfloat16)
     acts = motif_h
     offset = scatter_offset("tm", rows)
     part_rows = rows // lax.axis_size("tm")
     weight_part = lax.dynamic_slice_in_dim(weights, offset, part_rows, axis=0)
+    place = jnp.arange(width + rim, dtype=jnp.int32)[:, None]
+    lag_ids = jnp.arange(lags, dtype=jnp.int32)[None, :]
+    window = ((place >= rim - lag_ids) & (place < rim - lag_ids + width)).astype(jnp.bfloat16)
 
     def extend_padded(acts):
         hbf = acts.astype(jnp.bfloat16)
         before = from_behind(hbf[:, width - rim :], "tm", 1)
         return jnp.concatenate([before, hbf], axis=1)
 
-    def ratio_and_lagged(weight_bfloat, hext):
-        lagged_copies = stacked(hext, k_dev, rim, width)
-        part = (
-            lax.dot_general(
-                weight_bfloat, lagged_copies, reduce_over_rows, preferred_element_type=jnp.float32
-            )
-            * scale_factor
-        )
+    def ratio_of(weight_bfloat, hext):
+        part = recon_of(weight_bfloat, hext) * scale_factor
         estimated_counts = part + xor_swap(part, "motif", 1)
-        return ((spike_events / estimated_counts).astype(jnp.bfloat16), lagged_copies)
+        return (spike_events / estimated_counts).astype(jnp.bfloat16)
 
     bins = leading_bin + jnp.arange(width, dtype=jnp.int32)
     offsets = jnp.arange(lags, dtype=jnp.int32)
     mask = (bins[None, :] + offsets[:, None] < total_bins).astype(jnp.float32)
     hext = extend_padded(acts)
     for step in range(ITERS):
-        ratio, lagged_copies = ratio_and_lagged(weight_bfloat, hext)
+        ratio = ratio_of(weight_bfloat, hext)
         after = from_behind(ratio[:, :rim], "tm", -1)
         rext = jnp.concatenate([ratio, after], axis=1)
-        prod = jnp.dot(weight_bfloat, rext, preferred_element_type=jnp.float32).reshape(
-            k_dev, lags, width + rim
-        )
-        hnum = jnp.zeros((k_dev, width), jnp.float32)
-        for lag in range(lags):
-            hnum = hnum + prod[:, lag, lag : lag + width]
-        colsum = jnp.sum(weight_bfloat.reshape(k_dev, lags, n_dev), axis=2, dtype=jnp.float32)
+        hnum = hnum_of(weight_bfloat, rext)
+        colsum = jnp.sum(weight_bfloat, axis=2, dtype=jnp.float32)
         hnum, colsum = all_sum((hnum, colsum), "neuron")
         hden = jnp.dot(colsum, mask, precision=lax.Precision.HIGHEST)
         acts = acts * hnum / hden
         hext = extend_padded(acts)
-        ratio, lagged_copies = ratio_and_lagged(weight_bfloat, hext)
-        wnum = lax.dot_general(
-            lagged_copies, ratio, contract_cols, preferred_element_type=jnp.float32
-        )
-        wden = jnp.sum(lagged_copies, axis=1, dtype=jnp.float32)
+        ratio = ratio_of(weight_bfloat, hext)
+        wnum = wnum_of(hext, ratio).reshape(rows, n_dev)
+        wden = jnp.dot(hext, window, preferred_element_type=jnp.float32).reshape(rows)
         wnum = sum_scatter(wnum, "tm")
         wden = all_sum(wden, "tm")
         wden_part = lax.dynamic_slice_in_dim(wden, offset, part_rows, axis=0)
         weight_part = weight_part * wnum / wden_part[:, None]
         if step + 1 < ITERS:
-            weight_bfloat = gather_rows(weight_part.astype(jnp.bfloat16), "tm")
+            weight_bfloat = gather_rows(weight_part.astype(jnp.bfloat16), "tm").reshape(
+                k_dev, lags, n_dev
+            )
     weights = gather_rows(weight_part, "tm")
     return (weights.reshape(k_dev, lags, n_dev), acts)
 

time: 495 us -> 364 us (0.74); the launches traced: 485 us -> 360 us
  local copies, waits for them, and re-layouts: 132 us -> 16.6 us
  other arithmetic: 55.5 us -> 11.1 us
  matrix products: 27 us -> 57.9 us
  starting transfers between devices: 86.4 us -> 95 us
  waiting for transfers between devices: 183 us -> 178 us
    another operation x67 -> x0, local copies, waits for them, and re-layouts: 71.8 us -> none  [stacked(): return jnp.stack(rows, axis=1).reshape(count * (rim + 1), width)]
    conv_general_dilated x0 -> x8, matrix products: none -> 55.6 us  [the longest x2 29.1 us: wnum_of(): lax.conv_general_dilated(hext[None], ratio[None], (1,), [(0, 0)], dimensi...]
    slice x6 -> x2, local copies, waits for them, and re-layouts: 44.8 us -> 0.35 us  [sum_scatter(): low, high = (value[:half], value[half:])]
    dot_general x8 -> x2, matrix products: 23.5 us -> 0.55 us  [local(): jnp.dot(hext, window, preferred_element_type=jnp.float32).reshape(rows)]
    add x4 -> x1, other arithmetic: 22.8 us -> 0.01 us  [local(): rim - lag_ids + width]
    unnamed x124 -> x0, other arithmetic: 11.2 us -> none
    dot_general x1 -> x0, local copies, waits for them, and re-layouts: 9.7 us -> none  [local(): jnp.dot(weight_bfloat, rext, preferred_element_type=jnp.float32)]
    ppermute x34, starting transfers between devices: 60.9 us -> 69.4 us  [xor_swap(): lax.ppermute(value, axis, [(source, source ^ mask) for source in range(co...]
  transfers between devices with their start and end apart: 39 -> 39, of which waited for: 34 -> 34; matrix products, arithmetic and copies ran while one was open for 3% -> 2% of each run, Pallas kernels for 0% -> 0%
where the time goes in v2:
time: 364 us; the launch traced here: 360 us
  waiting for transfers between devices  178 us (49%)
  starting transfers between devices  95 us (26%)
  matrix products  57.9 us (16%)
  local copies, waits for them, and re-layouts  16.6 us (5%)
  other arithmetic  11.1 us (3%)
    ppermute x34, waiting for transfers between devices, xor_swap(): lax.ppermute(value, axis, [(source, source ^ mask) for source in range(co...  170 us
    ppermute x34, starting transfers between devices, xor_swap(): lax.ppermute(value, axis, [(source, source ^ mask) for source in range(co...  69.4 us
    conv_general_dilated x2, matrix products, wnum_of(): lax.conv_general_dilated(hext[None], ratio[None], (1,), [(0, 0)], dimensi...  29.1 us
    ppermute x5, starting transfers between devices, from_behind(): lax.ppermute(value, axis, [(source, source + steps) for source in range(f...  25.7 us
    conv_general_dilated x2, matrix products, hnum_of(): lax.conv_general_dilated(rext[None], weight_bfloat, (1,), [(0, 0)], dimen...  18.8 us
    conv_general_dilated x4, matrix products, recon_of(): lax.conv_general_dilated(hext[None], flipped, (1,), [(0, 0)], dimension_n...  7.71 us
  transfers between devices with their start and end apart: 39, of which 34 were waited for; matrix products, arithmetic and copies ran while one was open for 2% of the time, Pallas kernels for 0%

profile of v2, /device:TPU:1, one launch (start us, length us, event | category | flops | bytes accessed | tf_op | source)
XLA Modules:
  0.0 359.9 jit_solution(11141288712577807264)
XLA Ops:
  1.6 4.6 %collective-permute-start = (bf16[32,63]{1,0:T(8,128)(2,1)S(1)}, bf16[32,63]{1,0:T(8,128)(2,1)S(1)}, u32[]{:S(2)}, u32[]{:S(2)}) collective-permute-start(bf16[32,63]{1,0:T(8,128)(2,1)S(1)} %slice.100), channel_id=1, source_target_pairs={{0,16},{16,32},{32,48},{48,64},{64,80},{80,96},{96,112},{1,17},{17... | collective-permute-start | bytes 12104 | tf_op jit(solution)/shard_map/ppermute | solution.py:14
  15.4 21.0 %collective-permute-done.1 = f32[256,1024]{0,1:T(8,128)} collective-permute-done((f32[256,1024]{0,1:T(8,128)}, f32[256,1024]{0,1:T(8,128)}, u32[]{:S(2)}, u32[]{:S(2)}) %collective-permute-start.1) | collective-permute-done | bytes 1048608 | tf_op jit(solution)/shard_map/ppermute | solution.py:19
  40.0 4.4 %collective-permute-done.2 = bf16[256,63]{0,1:T(8,128)(2,1)S(1)} collective-permute-done((bf16[256,63]{0,1:T(8,128)(2,1)S(1)}, bf16[256,63]{0,1:T(8,128)(2,1)S(1)}, u32[]{:S(2)}, u32[]{:S(2)}) %collective-permute-start.2) | collective-permute-done | bytes 32288 | tf_op jit(solution)/shard_map/ppermute | solution.py:14
  44.7 9.4 %convolution_select_fusion.5 = f32[8,136,32]{2,0,1:T(8,128)S(1)} fusion(bf16[256,1,7,63]{0,2,3,1:T(8,128)(2,1)S(1)} %slice.104, bf16[256,1,8,136]{0,2,3,1:T(8,128)(2,1)S(1)} %copy.87, bf16[32,64,256]{2,1,0:T(8,128)(2,1)S(1)} %get-tuple-element.7, pred[8,136]{0,1:T(8,128)(4,1)S(1)} %copy-done.20), kind=kOutput, calls=%fused_computation.15 | convolution fusion | flops 1143330816 | bytes 1971776 | tf_op jit(solution)/shard_map/conv_general_dilated | solution.py:86
  54.7 3.5 collective-permute-start.3
  67.3 3.0 collective-permute-start.6
  74.9 3.2 collective-permute-done.8
  79.0 9.8 %collective-permute-start.9 = (bf16[32,63]{1,0:T(8,128)(2,1)S(1)}, bf16[32,63]{1,0:T(8,128)(2,1)S(1)}, u32[]{:S(2)}, u32[]{:S(2)}) collective-permute-start(bf16[32,63]{1,0:T(8,128)(2,1)S(1)} %slice.106), channel_id=1, source_target_pairs={{0,16},{16,32},{32,48},{48,64},{64,80},{80,96},{96,112},{1,17},{17... | collective-permute-start | bytes 12104 | tf_op jit(solution)/shard_map/ppermute | solution.py:14
  96.7 17.7 %collective-permute-done.10 = f32[256,1024]{0,1:T(8,128)S(1)} collective-permute-done((f32[256,1024]{0,1:T(8,128)}, f32[256,1024]{0,1:T(8,128)S(1)}, u32[]{:S(2)}, u32[]{:S(2)}) %collective-permute-start.10) | collective-permute-done | bytes 1048608 | tf_op jit(solution)/shard_map/ppermute | solution.py:19
  114.7 14.5 %fusion.8 = f32[32,64,256]{2,0,1:T(8,128)S(1)} fusion(bf16[1,32,1087]{1,0,2:T(2,128)(2,1)S(1)} %copy-done.6, bf16[1,256,1024]{1,2,0:T(8,128)(2,1)S(1)} %fusion.32), kind=kOutput, calls=%fused_computation.30 | convolution fusion | flops 1073741824 | bytes 2691008 | tf_op jit(solution)/shard_map/conv_general_dilated | solution.py:94
  133.2 6.8 %collective-permute-start.12 = (f32[512,256]{1,0:T(8,128)S(1)}, f32[512,256]{1,0:T(8,128)S(1)}, u32[]{:S(2)}, u32[]{:S(2)}) collective-permute-start(f32[512,256]{1,0:T(8,128)S(1)} %slice_select_fusion.1), channel_id=1, source_target_pairs={{0,32},{16,48},{32,0},{48,16},{64,96},{80,112},{96,64},{112,80},{1... | collective-permute-start | bytes 1572872 | tf_op jit(solution)/shard_map/ppermute | solution.py:19
  140.1 11.9 %collective-permute-done.12 = f32[512,256]{1,0:T(8,128)S(1)} collective-permute-done((f32[512,256]{1,0:T(8,128)S(1)}, f32[512,256]{1,0:T(8,128)S(1)}, u32[]{:S(2)}, u32[]{:S(2)}) %collective-permute-start.12) | collective-permute-done | bytes 524320 | tf_op jit(solution)/shard_map/ppermute | solution.py:19
  159.4 3.0 collective-permute-start.16
  165.2 3.0 collective-permute-start.17
  171.9 4.7 %collective-permute-done.18 = bf16[512,256]{1,0:T(8,128)(2,1)S(1)} collective-permute-done((bf16[512,256]{1,0:T(8,128)(2,1)S(1)}, bf16[512,256]{1,0:T(8,128)(2,1)S(1)}, u32[]{:S(2)}, u32[]{:S(2)}) %collective-permute-start.18) | collective-permute-done | bytes 262176 | tf_op jit(solution)/shard_map/ppermute | solution.py:19
  176.8 5.6 %collective-permute-start.19 = (bf16[1024,256]{1,0:T(8,128)(2,1)S(1)}, bf16[1024,256]{1,0:T(8,128)(2,1)S(1)}, u32[]{:S(2)}, u32[]{:S(2)}) collective-permute-start(bf16[1024,256]{1,0:T(8,128)(2,1)S(1)} %maximum_select_fusion.3), channel_id=1, source_target_pairs={{0,16},{16,0},{32,48},{48,32},{64,80},{80,64},{96,112},{112,96},{1... | collective-permute-start | bytes 1572872 | tf_op jit(solution)/shard_map/ppermute | solution.py:19
  187.8 23.4 %collective-permute-done.20 = f32[256,1024]{0,1:T(8,128)S(1)} collective-permute-done((f32[256,1024]{0,1:T(8,128)S(1)}, f32[256,1024]{0,1:T(8,128)S(1)}, u32[]{:S(2)}, u32[]{:S(2)}) %collective-permute-start.20) | collective-permute-done | bytes 1048608 | tf_op jit(solution)/shard_map/ppermute | solution.py:19
  211.4 3.5 collective-permute-start.21
  217.0 9.4 %convolution_select_fusion.4 = f32[8,136,32]{2,0,1:T(8,128)S(1)} fusion(bf16[256,1,7,63]{0,2,3,1:T(8,128)(2,1)S(1)} %slice.117, bf16[256,1,8,136]{0,2,3,1:T(8,128)(2,1)S(1)} %copy.101, bf16[32,64,256]{2,1,0:T(8,128)(2,1)S(1)} %bitcast.110, pred[8,136]{0,1:T(8,128)(4,1)S(1)} %copy-done.21), kind=kOutput, calls=%fused_computation.14 | convolution fusion | flops 1143330816 | bytes 1971776 | tf_op jit(solution)/shard_map/conv_general_dilated | solution.py:86
  226.9 3.4 collective-permute-start.22
  230.4 2.9 collective-permute-done.22
  233.5 5.0 %collective-permute-done.23 = f32[32,1024]{1,0:T(8,128)S(1)} collective-permute-done((f32[32,1024]{1,0:T(8,128)S(1)}, f32[32,1024]{1,0:T(8,128)S(1)}, u32[]{:S(2)}, u32[]{:S(2)}) %collective-permute-start.23) | collective-permute-done | bytes 131104 | tf_op jit(solution)/shard_map/ppermute | solution.py:19
  239.4 3.0 collective-permute-start.25
  251.2 5.6 %collective-permute-start.28 = (bf16[32,63]{1,0:T(8,128)(2,1)S(1)}, bf16[32,63]{1,0:T(8,128)(2,1)S(1)}, u32[]{:S(2)}, u32[]{:S(2)}) collective-permute-start(bf16[32,63]{1,0:T(8,128)(2,1)S(1)} %slice.119), channel_id=1, source_target_pairs={{0,16},{16,32},{32,48},{48,64},{64,80},{80,96},{96,112},{1,17},{17... | collective-permute-start | bytes 12104 | tf_op jit(solution)/shard_map/ppermute | solution.py:14
  264.7 22.4 %collective-permute-done.29 = f32[256,1024]{0,1:T(8,128)S(1)} collective-permute-done((f32[256,1024]{0,1:T(8,128)}, f32[256,1024]{0,1:T(8,128)S(1)}, u32[]{:S(2)}, u32[]{:S(2)}) %collective-permute-start.29) | collective-permute-done | bytes 1048608 | tf_op jit(solution)/shard_map/ppermute | solution.py:19
  287.3 14.6 %fusion.6 = f32[32,64,256]{2,0,1:T(8,128)S(1)} fusion(bf16[1,32,1087]{1,0,2:T(2,128)(2,1)S(1)} %copy-done.5, bf16[1,256,1024]{1,2,0:T(8,128)(2,1)S(1)} %fusion.33), kind=kOutput, calls=%fused_computation.28 | convolution fusion | flops 1073741824 | bytes 2691008 | tf_op jit(solution)/shard_map/conv_general_dilated | solution.py:94
  309.0 12.2 %collective-permute-done.31 = f32[512,256]{1,0:T(8,128)S(1)} collective-permute-done((f32[512,256]{1,0:T(8,128)S(1)}, f32[512,256]{1,0:T(8,128)S(1)}, u32[]{:S(2)}, u32[]{:S(2)}) %collective-permute-start.31) | collective-permute-done | bytes 524320 | tf_op jit(solution)/shard_map/ppermute | solution.py:19
  321.3 3.2 collective-permute-start.32
  327.2 2.9 collective-permute-done.34
  336.0 5.2 %collective-permute-done.36 = f32[256,256]{1,0:T(8,128)S(1)} collective-permute-done((f32[256,256]{1,0:T(8,128)S(1)}, f32[256,256]{1,0:T(8,128)S(1)}, u32[]{:S(2)}, u32[]{:S(2)}) %collective-permute-start.36) | collective-permute-done | bytes 262176 | tf_op jit(solution)/shard_map/ppermute | solution.py:19
  342.5 6.8 %collective-permute-done.37 = f32[512,256]{1,0:T(8,128)S(1)} collective-permute-done((f32[512,256]{1,0:T(8,128)S(1)}, f32[512,256]{1,0:T(8,128)S(1)}, u32[]{:S(2)}, u32[]{:S(2)}) %collective-permute-start.37) | collective-permute-done | bytes 524320 | tf_op jit(solution)/shard_map/ppermute | solution.py:19
  349.4 6.5 %collective-permute-start.38 = (f32[1024,256]{1,0:T(8,128)S(1)}, f32[1024,256]{1,0:T(8,128)S(1)}, u32[]{:S(2)}, u32[]{:S(2)}) collective-permute-start(f32[1024,256]{1,0:T(8,128)S(1)} %maximum_select_fusion.2), channel_id=1, source_target_pairs={{0,16},{16,0},{32,48},{48,32},{64,80},{80,64},{96,112},{112,96},{1... | collective-permute-start | bytes 3145736 | tf_op jit(solution)/shard_map/ppermute | solution.py:19
  (206 shorter events, 102.3 us)
Async XLA Ops:
  1.6 6.5 %collective-permute-start = (bf16[32,63]{1,0:T(8,128)(2,1)S(1)}, bf16[32,63]{1,0:T(8,128)(2,1)S(1)}, u32[]{:S(2)}, u32[]{:S(2)}) collective-permute-start(bf16[32,63]{1,0:T(8,128)(2,1)S(1)} %slice.100), channel_id=1, source_target_pairs={{0,16},{16,32},{32,48},{48,64},{64,80},{80,96},{96,112},{1,17},{17... | collective-permute-start | bytes 12104 | tf_op jit(solution)/shard_map/ppermute | solution.py:14
  12.2 24.2 %collective-permute-start.1 = (f32[256,1024]{0,1:T(8,128)}, f32[256,1024]{0,1:T(8,128)}, u32[]{:S(2)}, u32[]{:S(2)}) collective-permute-start(f32[256,1024]{0,1:T(8,128)} %slice_bitcast_fusion.3), channel_id=1, source_target_pairs={{0,1},{1,0},{2,3},{3,2},{4,5},{5,4},{6,7},{7,6},{8,9},{9,8},{10,11... | collective-permute-start | bytes 3145736 | tf_op jit(solution)/shard_map/ppermute | solution.py:19
  37.9 6.5 %collective-permute-start.2 = (bf16[256,63]{0,1:T(8,128)(2,1)S(1)}, bf16[256,63]{0,1:T(8,128)(2,1)S(1)}, u32[]{:S(2)}, u32[]{:S(2)}) collective-permute-start(bf16[256,63]{0,1:T(8,128)(2,1)S(1)} %slice.103), channel_id=1, source_target_pairs={{16,0},{32,16},{48,32},{64,48},{80,64},{96,80},{112,96},{17,1},{33... | collective-permute-start | bytes 96776 | tf_op jit(solution)/shard_map/ppermute | solution.py:14
  54.7 5.9 %collective-permute-start.3 = (f32[32,1024]{1,0:T(8,128)S(1)}, f32[32,1024]{1,0:T(8,128)S(1)}, u32[]{:S(2)}, u32[]{:S(2)}) collective-permute-start(f32[32,1024]{1,0:T(8,128)S(1)} %slice_bitcast_fusion.5), channel_id=1, source_target_pairs={{0,2},{2,0},{4,6},{6,4},{8,10},{10,8},{12,14},{14,12},{1,3},{3,1},... | collective-permute-start | bytes 393224 | tf_op jit(solution)/shard_map/ppermute | solution.py:19
  60.6 3.9 %collective-permute-start.4 = (f32[32,1024]{1,0:T(8,128)S(1)}, f32[32,1024]{1,0:T(8,128)S(1)}, u32[]{:S(2)}, u32[]{:S(2)}) collective-permute-start(f32[32,1024]{1,0:T(8,128)S(1)} %fusion.98), channel_id=1, source_target_pairs={{0,4},{2,6},{4,0},{6,2},{8,12},{10,14},{12,8},{14,10},{1,5},{3,7},... | collective-permute-start | bytes 393224 | tf_op jit(solution)/shard_map/ppermute | solution.py:19
  64.5 13.6 %collective-permute-start.5 = (f32[32,1024]{1,0:T(8,128)S(1)}, f32[32,1024]{1,0:T(8,128)S(1)}, u32[]{:S(2)}, u32[]{:S(2)}) collective-permute-start(f32[32,1024]{1,0:T(8,128)S(1)} %add.160), channel_id=1, source_target_pairs={{0,8},{2,10},{4,12},{6,14},{8,0},{10,2},{12,4},{14,6},{1,9},{3,11}... | collective-permute-start | bytes 393224 | tf_op jit(solution)/shard_map/ppermute | solution.py:19
  67.3 4.1 %collective-permute-start.6 = (f32[32,64]{1,0:T(8,128)S(1)}, f32[32,64]{1,0:T(8,128)S(1)}, u32[]{:S(2)}, u32[]{:S(2)}) collective-permute-start(f32[32,64]{1,0:T(8,128)S(1)} %get-tuple-element.6), channel_id=1, source_target_pairs={{0,2},{2,0},{4,6},{6,4},{8,10},{10,8},{12,14},{14,12},{1,3},{3,1},... | collective-permute-start | bytes 24584 | tf_op jit(solution)/shard_map/ppermute | solution.py:19
  74.0 4.1 %collective-permute-start.8 = (f32[32,64]{1,0:T(8,128)S(1)}, f32[32,64]{1,0:T(8,128)S(1)}, u32[]{:S(2)}, u32[]{:S(2)}) collective-permute-start(f32[32,64]{1,0:T(8,128)S(1)} %add.163), channel_id=1, source_target_pairs={{0,8},{2,10},{4,12},{6,14},{8,0},{10,2},{12,4},{14,6},{1,9},{3,11}... | collective-permute-start | bytes 24584 | tf_op jit(solution)/shard_map/ppermute | solution.py:19
  79.0 10.1 %collective-permute-start.9 = (bf16[32,63]{1,0:T(8,128)(2,1)S(1)}, bf16[32,63]{1,0:T(8,128)(2,1)S(1)}, u32[]{:S(2)}, u32[]{:S(2)}) collective-permute-start(bf16[32,63]{1,0:T(8,128)(2,1)S(1)} %slice.106), channel_id=1, source_target_pairs={{0,16},{16,32},{32,48},{48,64},{64,80},{80,96},{96,112},{1,17},{17... | collective-permute-start | bytes 12104 | tf_op jit(solution)/shard_map/ppermute | solution.py:14
  94.3 20.2 %collective-permute-start.10 = (f32[256,1024]{0,1:T(8,128)}, f32[256,1024]{0,1:T(8,128)S(1)}, u32[]{:S(2)}, u32[]{:S(2)}) collective-permute-start(f32[256,1024]{0,1:T(8,128)} %slice_bitcast_fusion.2), channel_id=1, source_target_pairs={{0,1},{1,0},{2,3},{3,2},{4,5},{5,4},{6,7},{7,6},{8,9},{9,8},{10,11... | collective-permute-start | bytes 3145736 | tf_op jit(solution)/shard_map/ppermute | solution.py:19
  133.2 18.8 %collective-permute-start.12 = (f32[512,256]{1,0:T(8,128)S(1)}, f32[512,256]{1,0:T(8,128)S(1)}, u32[]{:S(2)}, u32[]{:S(2)}) collective-permute-start(f32[512,256]{1,0:T(8,128)S(1)} %slice_select_fusion.1), channel_id=1, source_target_pairs={{0,32},{16,48},{32,0},{48,16},{64,96},{80,112},{96,64},{112,80},{1... | collective-permute-start | bytes 1572872 | tf_op jit(solution)/shard_map/ppermute | solution.py:19
  152.1 11.3 %collective-permute-start.13 = (f32[256,256]{1,0:T(8,128)S(1)}, f32[256,256]{1,0:T(8,128)S(1)}, u32[]{:S(2)}, u32[]{:S(2)}) collective-permute-start(f32[256,256]{1,0:T(8,128)S(1)} %slice_select_fusion.3), channel_id=1, source_target_pairs={{0,64},{16,80},{32,96},{48,112},{64,0},{80,16},{96,32},{112,48},{1... | collective-permute-start | bytes 786440 | tf_op jit(solution)/shard_map/ppermute | solution.py:19
  159.4 4.0 %collective-permute-start.16 = (f32[2048]{0:T(1024)S(1)}, f32[2048]{0:T(1024)S(1)}, u32[]{:S(2)}, u32[]{:S(2)}) collective-permute-start(f32[2048]{0:T(1024)S(1)} %add.177), channel_id=1, source_target_pairs={{0,64},{16,80},{32,96},{48,112},{64,0},{80,16},{96,32},{112,48},{1... | collective-permute-start | bytes 24584 | tf_op jit(solution)/shard_map/ppermute | solution.py:19
  165.2 5.3 %collective-permute-start.17 = (bf16[256,256]{1,0:T(8,128)(2,1)S(1)}, bf16[256,256]{1,0:T(8,128)(2,1)S(1)}, u32[]{:S(2)}, u32[]{:S(2)}) collective-permute-start(bf16[256,256]{1,0:T(8,128)(2,1)S(1)} %get-tuple-element.4), channel_id=1, source_target_pairs={{0,64},{16,80},{32,96},{48,112},{64,0},{80,16},{96,32},{112,48},{1... | collective-permute-start | bytes 393224 | tf_op jit(solution)/shard_map/ppermute | solution.py:19
  170.6 5.9 %collective-permute-start.18 = (bf16[512,256]{1,0:T(8,128)(2,1)S(1)}, bf16[512,256]{1,0:T(8,128)(2,1)S(1)}, u32[]{:S(2)}, u32[]{:S(2)}) collective-permute-start(bf16[512,256]{1,0:T(8,128)(2,1)S(1)} %maximum_select_fusion.5), channel_id=1, source_target_pairs={{0,32},{16,48},{32,0},{48,16},{64,96},{80,112},{96,64},{112,80},{1... | collective-permute-start | bytes 786440 | tf_op jit(solution)/shard_map/ppermute | solution.py:19
  176.8 7.1 %collective-permute-start.19 = (bf16[1024,256]{1,0:T(8,128)(2,1)S(1)}, bf16[1024,256]{1,0:T(8,128)(2,1)S(1)}, u32[]{:S(2)}, u32[]{:S(2)}) collective-permute-start(bf16[1024,256]{1,0:T(8,128)(2,1)S(1)} %maximum_select_fusion.3), channel_id=1, source_target_pairs={{0,16},{16,0},{32,48},{48,32},{64,80},{80,64},{96,112},{112,96},{1... | collective-permute-start | bytes 1572872 | tf_op jit(solution)/shard_map/ppermute | solution.py:19
  186.7 24.4 %collective-permute-start.20 = (f32[256,1024]{0,1:T(8,128)S(1)}, f32[256,1024]{0,1:T(8,128)S(1)}, u32[]{:S(2)}, u32[]{:S(2)}) collective-permute-start(f32[256,1024]{0,1:T(8,128)S(1)} %slice_bitcast_fusion.1), channel_id=1, source_target_pairs={{0,1},{1,0},{2,3},{3,2},{4,5},{5,4},{6,7},{7,6},{8,9},{9,8},{10,11... | collective-permute-start | bytes 3145736 | tf_op jit(solution)/shard_map/ppermute | solution.py:19
  211.4 5.2 %collective-permute-start.21 = (bf16[256,63]{0,1:T(8,128)(2,1)S(1)}, bf16[256,63]{0,1:T(8,128)(2,1)S(1)}, u32[]{:S(2)}, u32[]{:S(2)}) collective-permute-start(bf16[256,63]{0,1:T(8,128)(2,1)S(1)} %slice.116), channel_id=1, source_target_pairs={{16,0},{32,16},{48,32},{64,48},{80,64},{96,80},{112,96},{17,1},{33... | collective-permute-start | bytes 96776 | tf_op jit(solution)/shard_map/ppermute | solution.py:14
  226.9 6.4 %collective-permute-start.22 = (f32[32,1024]{1,0:T(8,128)S(1)}, f32[32,1024]{1,0:T(8,128)S(1)}, u32[]{:S(2)}, u32[]{:S(2)}) collective-permute-start(f32[32,1024]{1,0:T(8,128)S(1)} %slice_bitcast_fusion.4), channel_id=1, source_target_pairs={{0,2},{2,0},{4,6},{6,4},{8,10},{10,8},{12,14},{14,12},{1,3},{3,1},... | collective-permute-start | bytes 393224 | tf_op jit(solution)/shard_map/ppermute | solution.py:19
  233.3 5.3 %collective-permute-start.23 = (f32[32,1024]{1,0:T(8,128)S(1)}, f32[32,1024]{1,0:T(8,128)S(1)}, u32[]{:S(2)}, u32[]{:S(2)}) collective-permute-start(f32[32,1024]{1,0:T(8,128)S(1)} %fusion.99), channel_id=1, source_target_pairs={{0,4},{2,6},{4,0},{6,2},{8,12},{10,14},{12,8},{14,10},{1,5},{3,7},... | collective-permute-start | bytes 393224 | tf_op jit(solution)/shard_map/ppermute | solution.py:19
  238.6 11.6 %collective-permute-start.24 = (f32[32,1024]{1,0:T(8,128)S(1)}, f32[32,1024]{1,0:T(8,128)S(1)}, u32[]{:S(2)}, u32[]{:S(2)}) collective-permute-start(f32[32,1024]{1,0:T(8,128)S(1)} %add.181), channel_id=1, source_target_pairs={{0,8},{2,10},{4,12},{6,14},{8,0},{10,2},{12,4},{14,6},{1,9},{3,11}... | collective-permute-start | bytes 393224 | tf_op jit(solution)/shard_map/ppermute | solution.py:19
  239.4 4.1 %collective-permute-start.25 = (f32[32,64]{1,0:T(8,128)S(1)}, f32[32,64]{1,0:T(8,128)S(1)}, u32[]{:S(2)}, u32[]{:S(2)}) collective-permute-start(f32[32,64]{1,0:T(8,128)S(1)} %reduce_sum.22), channel_id=1, source_target_pairs={{0,2},{2,0},{4,6},{6,4},{8,10},{10,8},{12,14},{14,12},{1,3},{3,1},... | collective-permute-start | bytes 24584 | tf_op jit(solution)/shard_map/ppermute | solution.py:19
  246.1 4.1 %collective-permute-start.27 = (f32[32,64]{1,0:T(8,128)S(1)}, f32[32,64]{1,0:T(8,128)S(1)}, u32[]{:S(2)}, u32[]{:S(2)}) collective-permute-start(f32[32,64]{1,0:T(8,128)S(1)} %add.184), channel_id=1, source_target_pairs={{0,8},{2,10},{4,12},{6,14},{8,0},{10,2},{12,4},{14,6},{1,9},{3,11}... | collective-permute-start | bytes 24584 | tf_op jit(solution)/shard_map/ppermute | solution.py:19
  251.2 6.4 %collective-permute-start.28 = (bf16[32,63]{1,0:T(8,128)(2,1)S(1)}, bf16[32,63]{1,0:T(8,128)(2,1)S(1)}, u32[]{:S(2)}, u32[]{:S(2)}) collective-permute-start(bf16[32,63]{1,0:T(8,128)(2,1)S(1)} %slice.119), channel_id=1, source_target_pairs={{0,16},{16,32},{32,48},{48,64},{64,80},{80,96},{96,112},{1,17},{17... | collective-permute-start | bytes 12104 | tf_op jit(solution)/shard_map/ppermute | solution.py:14
  262.0 25.0 %collective-permute-start.29 = (f32[256,1024]{0,1:T(8,128)}, f32[256,1024]{0,1:T(8,128)S(1)}, u32[]{:S(2)}, u32[]{:S(2)}) collective-permute-start(f32[256,1024]{0,1:T(8,128)} %slice_bitcast_fusion), channel_id=1, source_target_pairs={{0,1},{1,0},{2,3},{3,2},{4,5},{5,4},{6,7},{7,6},{8,9},{9,8},{10,11... | collective-permute-start | bytes 3145736 | tf_op jit(solution)/shard_map/ppermute | solution.py:19
  302.9 3.2 collective-permute-start.30
  306.3 14.8 %collective-permute-start.31 = (f32[512,256]{1,0:T(8,128)S(1)}, f32[512,256]{1,0:T(8,128)S(1)}, u32[]{:S(2)}, u32[]{:S(2)}) collective-permute-start(f32[512,256]{1,0:T(8,128)S(1)} %slice_select_fusion), channel_id=1, source_target_pairs={{0,32},{16,48},{32,0},{48,16},{64,96},{80,112},{96,64},{112,80},{1... | collective-permute-start | bytes 1572872 | tf_op jit(solution)/shard_map/ppermute | solution.py:19
  321.3 12.9 %collective-permute-start.32 = (f32[256,256]{1,0:T(8,128)S(1)}, f32[256,256]{1,0:T(8,128)S(1)}, u32[]{:S(2)}, u32[]{:S(2)}) collective-permute-start(f32[256,256]{1,0:T(8,128)S(1)} %slice_select_fusion.2), channel_id=1, source_target_pairs={{0,64},{16,80},{32,96},{48,112},{64,0},{80,16},{96,32},{112,48},{1... | collective-permute-start | bytes 786440 | tf_op jit(solution)/shard_map/ppermute | solution.py:19
  330.1 4.0 %collective-permute-start.35 = (f32[2048]{0:T(1024)S(1)}, f32[2048]{0:T(1024)S(1)}, u32[]{:S(2)}, u32[]{:S(2)}) collective-permute-start(f32[2048]{0:T(1024)S(1)} %add.191), channel_id=1, source_target_pairs={{0,64},{16,80},{32,96},{48,112},{64,0},{80,16},{96,32},{112,48},{1... | collective-permute-start | bytes 24584 | tf_op jit(solution)/shard_map/ppermute | solution.py:19
  334.3 6.8 %collective-permute-start.36 = (f32[256,256]{1,0:T(8,128)S(1)}, f32[256,256]{1,0:T(8,128)S(1)}, u32[]{:S(2)}, u32[]{:S(2)}) collective-permute-start(f32[256,256]{1,0:T(8,128)S(1)} %multiply_divide_fusion), channel_id=1, source_target_pairs={{0,64},{16,80},{32,96},{48,112},{64,0},{80,16},{96,32},{112,48},{1... | collective-permute-start | bytes 786440 | tf_op jit(solution)/shard_map/ppermute | solution.py:19
  341.2 8.1 %collective-permute-start.37 = (f32[512,256]{1,0:T(8,128)S(1)}, f32[512,256]{1,0:T(8,128)S(1)}, u32[]{:S(2)}, u32[]{:S(2)}) collective-permute-start(f32[512,256]{1,0:T(8,128)S(1)} %maximum_select_fusion.4), channel_id=1, source_target_pairs={{0,32},{16,48},{32,0},{48,16},{64,96},{80,112},{96,64},{112,80},{1... | collective-permute-start | bytes 1572872 | tf_op jit(solution)/shard_map/ppermute | solution.py:19
  349.4 8.8 %collective-permute-start.38 = (f32[1024,256]{1,0:T(8,128)S(1)}, f32[1024,256]{1,0:T(8,128)S(1)}, u32[]{:S(2)}, u32[]{:S(2)}) collective-permute-start(f32[1024,256]{1,0:T(8,128)S(1)} %maximum_select_fusion.2), channel_id=1, source_target_pairs={{0,16},{16,0},{32,48},{48,32},{64,80},{80,64},{96,112},{112,96},{1... | collective-permute-start | bytes 3145736 | tf_op jit(solution)/shard_map/ppermute | solution.py:19
  (34 other events, 454.6 us)

commit v3 on v2

--- a/solution.py
+++ b/solution.py
@@ -59,14 +59,23 @@
     return offset
 
 
-def gather_rows(value, axis):
+def gather_rows(value, axis, dim=0):
     for mask in reversed(masks_of(axis)):
         other = xor_swap(value, axis, mask)
         upper = bit_of(axis, mask)
         value = jnp.where(
-            upper, jnp.concatenate([other, value], axis=0), jnp.concatenate([value, other], axis=0)
+            upper,
+            jnp.concatenate([other, value], axis=dim),
+            jnp.concatenate([value, other], axis=dim),
         )
     return value
+
+
+def from_behind_other(value, steps):
+    count = lax.axis_size("tm")
+    pairs = [(2 * source + side, 2 * (source + steps) + 1 - side)
+             for source in range(count - steps) for side in range(2)]
+    return lax.ppermute(value, ("tm", "motif"), pairs)
 
 
 CONV_DIMS = lax.ConvDimensionNumbers
@@ -109,6 +118,7 @@
     spike_events = counts.astype(jnp.float32)
     weights = motif_w.reshape(rows, n_dev)
     weight_bfloat = motif_w.astype(jnp.bfloat16)
+    weight_all = jnp.concatenate([weight_bfloat, xor_swap(weight_bfloat, "motif", 1)], axis=0)
     acts = motif_h
     offset = scatter_offset("tm", rows)
     part_rows = rows // lax.axis_size("tm")
@@ -119,20 +129,23 @@
 
     def extend_padded(acts):
         hbf = acts.astype(jnp.bfloat16)
-        before = from_behind(hbf[:, width - rim :], "tm", 1)
-        return jnp.concatenate([before, hbf], axis=1)
+        tail = hbf[:, width - rim :]
+        own = jnp.concatenate([from_behind(tail, "tm", 1), hbf], axis=1)
+        other = jnp.concatenate(
+            [from_behind_other(tail, 1), xor_swap(hbf, "motif", 1)], axis=1
+        )
+        return own, jnp.concatenate([own, other], axis=0)
 
-    def ratio_of(weight_bfloat, hext):
-        part = recon_of(weight_bfloat, hext) * scale_factor
-        estimated_counts = part + xor_swap(part, "motif", 1)
+    def ratio_of(weight_all, hext_all):
+        estimated_counts = recon_of(weight_all, hext_all) * scale_factor
         return (spike_events / estimated_counts).astype(jnp.bfloat16)
 
     bins = leading_bin + jnp.arange(width, dtype=jnp.int32)
     offsets = jnp.arange(lags, dtype=jnp.int32)
     mask = (bins[None, :] + offsets[:, None] < total_bins).astype(jnp.float32)
-    hext = extend_padded(acts)
+    hext, hext_all = extend_padded(acts)
     for step in range(ITERS):
-        ratio = ratio_of(weight_bfloat, hext)
+        ratio = ratio_of(weight_all, hext_all)
         after = from_behind(ratio[:, :rim], "tm", -1)
         rext = jnp.concatenate([ratio, after], axis=1)
         hnum = hnum_of(weight_bfloat, rext)
@@ -140,8 +153,8 @@
         hnum, colsum = all_sum((hnum, colsum), "neuron")
         hden = jnp.dot(colsum, mask, precision=lax.Precision.HIGHEST)
         acts = acts * hnum / hden
-        hext = extend_padded(acts)
-        ratio = ratio_of(weight_bfloat, hext)
+        hext, hext_all = extend_padded(acts)
+        ratio = ratio_of(weight_all, hext_all)
         wnum = wnum_of(hext, ratio).reshape(rows, n_dev)
         wden = jnp.dot(hext, window, preferred_element_type=jnp.float32).reshape(rows)
         wnum = sum_scatter(wnum, "tm")
@@ -149,9 +162,11 @@
         wden_part = lax.dynamic_slice_in_dim(wden, offset, part_rows, axis=0)
         weight_part = weight_part * wnum / wden_part[:, None]
         if step + 1 < ITERS:
-            weight_bfloat = gather_rows(weight_part.astype(jnp.bfloat16), "tm").reshape(
-                k_dev, lags, n_dev
-            )
+            part_bfloat = weight_part.astype(jnp.bfloat16)
+            pair = jnp.stack([part_bfloat, xor_swap(part_bfloat, "motif", 1)], axis=0)
+            pair = gather_rows(pair, "tm", dim=1)
+            weight_all = pair.reshape(2 * k_dev, lags, n_dev)
+            weight_bfloat = weight_all[:k_dev]
     weights = gather_rows(weight_part, "tm")
     return (weights.reshape(k_dev, lags, n_dev), acts)
 

time: 364 us -> 319 us (0.88)
  waiting for transfers between devices: 178 us -> 121 us
  matrix products: 57.9 us -> 66.8 us
    ppermute x34 -> x35, waiting for transfers between devices: 170 us -> 98.4 us  [xor_swap(): lax.ppermute(value, axis, [(source, source ^ mask) for source in range(co...]
    ppermute x0 -> x3, waiting for transfers between devices: none -> 17.7 us  [from_behind_other(): return lax.ppermute(value, ('tm', 'motif'), pairs)]
    ppermute x0 -> x3, starting transfers between devices: none -> 10.3 us  [from_behind_other(): return lax.ppermute(value, ('tm', 'motif'), pairs)]
    conv_general_dilated x4, matrix products: 7.71 us -> 14.6 us  [recon_of(): lax.conv_general_dilated(hext[None], flipped, (1,), [(0, 0)], dimension_n...]
    ppermute x5, starting transfers between devices: 25.7 us -> 21.8 us  [from_behind(): lax.ppermute(value, axis, [(source, source + steps) for source in range(f...]
    ppermute x34 -> x35, starting transfers between devices: 69.4 us -> 66.1 us  [xor_swap(): lax.ppermute(value, axis, [(source, source ^ mask) for source in range(co...]
  transfers between devices with their start and end apart: 39 -> 43, of which waited for: 34 -> 34; matrix products, arithmetic and copies ran while one was open for 2% -> 2% of each run, Pallas kernels for 0% -> 0%
where the time goes in v3:
time: 319 us; the launch traced here: 314 us
  waiting for transfers between devices  121 us (38%)
  starting transfers between devices  98.1 us (31%)
  matrix products  66.8 us (21%)
  local copies, waits for them, and re-layouts  15.4 us (5%)
  other arithmetic  10.6 us (3%)
    ppermute x35, waiting for transfers between devices, xor_swap(): lax.ppermute(value, axis, [(source, source ^ mask) for source in range(co...  98.4 us
    ppermute x35, starting transfers between devices, xor_swap(): lax.ppermute(value, axis, [(source, source ^ mask) for source in range(co...  66.1 us
    conv_general_dilated x2, matrix products, wnum_of(): lax.conv_general_dilated(hext[None], ratio[None], (1,), [(0, 0)], dimensi...  29.1 us
    ppermute x5, starting transfers between devices, from_behind(): lax.ppermute(value, axis, [(source, source + steps) for source in range(f...  21.8 us
    conv_general_dilated x2, matrix products, hnum_of(): lax.conv_general_dilated(rext[None], weight_bfloat, (1,), [(0, 0)], dimen...  19.8 us
    ppermute x3, waiting for transfers between devices, from_behind_other(): return lax.ppermute(value, ('tm', 'motif'), pairs)  17.7 us
    conv_general_dilated x4, matrix products, recon_of(): lax.conv_general_dilated(hext[None], flipped, (1,), [(0, 0)], dimension_n...  14.6 us
    ppermute x3, starting transfers between devices, from_behind_other(): return lax.ppermute(value, ('tm', 'motif'), pairs)  10.3 us
  transfers between devices with their start and end apart: 43, of which 34 were waited for; matrix products, arithmetic and copies ran while one was open for 2% of the time, Pallas kernels for 0%

profile of v3, /device:TPU:1, one launch (start us, length us, event | category | flops | bytes accessed | tf_op | source)
XLA Modules:
  0.0 314.0 jit_solution(17361637826508637625)
XLA Ops:
  0.6 3.0 convert_reduce_fusion.1
  6.4 5.5 %collective-permute-start.1 = (bf16[32,63]{1,0:T(8,128)(2,1)S(1)}, bf16[32,63]{1,0:T(8,128)(2,1)S(1)}, u32[]{:S(2)}, u32[]{:S(2)}) collective-permute-start(bf16[32,63]{1,0:T(8,128)(2,1)S(1)} %slice.108), channel_id=1, source_target_pairs={{0,17},{1,16},{16,33},{17,32},{32,49},{33,48},{48,65},{49,64},{64,... | collective-permute-start | bytes 12104 | tf_op jit(solution)/shard_map/ppermute | solution.py:78
  14.1 17.2 %collective-permute-done.1 = bf16[32,63]{1,0:T(8,128)(2,1)S(1)} collective-permute-done((bf16[32,63]{1,0:T(8,128)(2,1)S(1)}, bf16[32,63]{1,0:T(8,128)(2,1)S(1)}, u32[]{:S(2)}, u32[]{:S(2)}) %collective-permute-start.1) | collective-permute-done | bytes 4064 | tf_op jit(solution)/shard_map/ppermute | solution.py:78
  32.2 3.8 %fusion.9 = f32[8,136,256]{2,0,1:T(8,128)S(1)} fusion(bf16[32,64,256]{2,0,1:T(8,128)(2,1)} %collective-permute-done.3, bf16[32,64,256]{2,0,1:T(8,128)(2,1)S(1)} %get-tuple-element.5, pred[8,136]{0,1:T(8,128)(4,1)S(1)} %copy-done.21, bf16[64,1,7,63]{0,2,3,1:T(8,128)(2,1)S(1)} %slice.109, bf16[64,1,8,136]{0,2,3,1:T(8,128)(2,1)S(1)} %copy.45), kind=kOutput, calls=%fused_computation.16 | convolution fusion | flops 2287064064 | bytes 3408064 | tf_op jit(solution)/shard_map/conv_general_dilated | solution.py:87
  42.0 9.3 %convolution_select_fusion.1 = f32[8,136,32]{2,0,1:T(8,128)S(1)} fusion(bf16[32,64,256]{2,0,1:T(8,128)(2,1)S(1)} %get-tuple-element.5, bf16[256,1,7,63]{0,2,3,1:T(8,128)(2,1)S(1)} %slice.112, bf16[256,1,8,136]{0,2,3,1:T(8,128)(2,1)S(1)} %copy.49, pred[8,136]{0,1:T(8,128)(4,1)S(1)} %copy-done.21), kind=kOutput, calls=%fused_computation.24 | convolution fusion | flops 1143330816 | bytes 1971776 | tf_op jit(solution)/shard_map/conv_general_dilated | solution.py:95
  51.9 3.5 %collective-permute-start.5 = (f32[32,1024]{1,0:T(8,128)S(1)}, f32[32,1024]{1,0:T(8,128)S(1)}, u32[]{:S(2)}, u32[]{:S(2)}) collective-permute-start(f32[32,1024]{1,0:T(8,128)S(1)} %slice_bitcast_fusion.5), channel_id=1, source_target_pairs={{0,2},{2,0},{4,6},{6,4},{8,10},{10,8},{12,14},{14,12},{1,3},{3,1},... | collective-permute-start | bytes 393224 | tf_op jit(solution)/shard_map/ppermute | solution.py:19
  59.1 3.6 %collective-permute-done.6 = f32[32,1024]{1,0:T(8,128)S(1)} collective-permute-done((f32[32,1024]{1,0:T(8,128)S(1)}, f32[32,1024]{1,0:T(8,128)S(1)}, u32[]{:S(2)}, u32[]{:S(2)}) %collective-permute-start.6) | collective-permute-done | bytes 131104 | tf_op jit(solution)/shard_map/ppermute | solution.py:19
  65.5 3.5 %collective-permute-start.8 = (f32[32,64]{0,1:T(8,128)S(1)}, f32[32,64]{0,1:T(8,128)S(1)}, u32[]{:S(2)}, u32[]{:S(2)}) collective-permute-start(f32[32,64]{0,1:T(8,128)S(1)} %get-tuple-element.4), channel_id=1, source_target_pairs={{0,2},{2,0},{4,6},{6,4},{8,10},{10,8},{12,14},{14,12},{1,3},{3,1},... | collective-permute-start | bytes 24584 | tf_op jit(solution)/shard_map/ppermute | solution.py:19
  74.0 3.4 %collective-permute-done.10 = f32[32,64]{0,1:T(8,128)S(1)} collective-permute-done((f32[32,64]{0,1:T(8,128)S(1)}, f32[32,64]{0,1:T(8,128)S(1)}, u32[]{:S(2)}, u32[]{:S(2)}) %collective-permute-start.10) | collective-permute-done | bytes 8224 | tf_op jit(solution)/shard_map/ppermute | solution.py:19
  78.4 7.8 %collective-permute-start.11 = (bf16[32,63]{1,0:T(8,128)(2,1)S(1)}, bf16[32,63]{1,0:T(8,128)(2,1)S(1)}, u32[]{:S(2)}, u32[]{:S(2)}) collective-permute-start(bf16[32,63]{1,0:T(8,128)(2,1)S(1)} %slice.114), channel_id=1, source_target_pairs={{0,16},{16,32},{32,48},{48,64},{64,80},{80,96},{96,112},{1,17},{17... | collective-permute-start | bytes 12104 | tf_op jit(solution)/shard_map/ppermute | solution.py:14
  93.2 3.9 %fusion.11 = f32[8,136,256]{2,0,1:T(8,128)S(1)} fusion(bf16[32,64,256]{2,0,1:T(8,128)(2,1)} %collective-permute-done.3, bf16[32,64,256]{2,0,1:T(8,128)(2,1)S(1)} %get-tuple-element.5, pred[8,136]{0,1:T(8,128)(4,1)S(1)} %copy-done.21, bf16[64,1,7,63]{0,2,3,1:T(8,128)(2,1)S(1)} %slice.115, bf16[64,1,8,136]{0,2,3,1:T(8,128)(2,1)S(1)} %copy.52), kind=kOutput, calls=%fused_computation.18 | convolution fusion | flops 2287064064 | bytes 3408064 | tf_op jit(solution)/shard_map/conv_general_dilated | solution.py:87
  97.6 14.5 %fusion.35 = f32[32,64,256]{2,0,1:T(8,128)S(1)} fusion(bf16[1,32,1087]{1,0,2:T(2,128)(2,1)S(1)} %copy.54, bf16[1,256,1024]{1,2,0:T(8,128)(2,1)S(1)} %fusion.53), kind=kOutput, calls=%fused_computation.44 | convolution fusion | flops 1073741824 | bytes 2691008 | tf_op jit(solution)/shard_map/conv_general_dilated | solution.py:103
  119.1 11.7 %collective-permute-done.15 = f32[512,256]{1,0:T(8,128)S(1)} collective-permute-done((f32[512,256]{1,0:T(8,128)S(1)}, f32[512,256]{1,0:T(8,128)S(1)}, u32[]{:S(2)}, u32[]{:S(2)}) %collective-permute-start.15) | collective-permute-done | bytes 524320 | tf_op jit(solution)/shard_map/ppermute | solution.py:19
  135.1 3.0 collective-permute-done.18
  138.1 3.3 %collective-permute-start.19 = (f32[2048]{0:T(1024)S(1)}, f32[2048]{0:T(1024)S(1)}, u32[]{:S(2)}, u32[]{:S(2)}) collective-permute-start(f32[2048]{0:T(1024)S(1)} %add.163), channel_id=1, source_target_pairs={{0,64},{16,80},{32,96},{48,112},{64,0},{80,16},{96,32},{112,48},{1... | collective-permute-start | bytes 24584 | tf_op jit(solution)/shard_map/ppermute | solution.py:19
  144.4 3.7 %collective-permute-done.20 = bf16[256,256]{1,0:T(8,128)(2,1)S(1)} collective-permute-done((bf16[256,256]{1,0:T(8,128)(2,1)S(1)}, bf16[256,256]{1,0:T(8,128)(2,1)S(1)}, u32[]{:S(2)}, u32[]{:S(2)}) %collective-permute-start.20) | collective-permute-done | bytes 131104 | tf_op jit(solution)/shard_map/ppermute | solution.py:19
  148.1 3.0 collective-permute-start.21
  151.1 3.8 %collective-permute-done.21 = bf16[2,256,256]{2,1,0:T(8,128)(2,1)S(1)} collective-permute-done((bf16[2,256,256]{2,1,0:T(8,128)(2,1)S(1)}, bf16[2,256,256]{2,1,0:T(8,128)(2,1)S(1)}, u32[]{:S(2)}, u32[]{:S(2)}) %collective-permute-start.21) | collective-permute-done | bytes 262176 | tf_op jit(solution)/shard_map/ppermute | solution.py:19
  156.0 10.4 %collective-permute-done.22 = bf16[2,512,256]{2,1,0:T(8,128)(2,1)S(1)} collective-permute-done((bf16[2,512,256]{2,1,0:T(8,128)(2,1)S(1)}, bf16[2,512,256]{2,1,0:T(8,128)(2,1)S(1)}, u32[]{:S(2)}, u32[]{:S(2)}) %collective-permute-start.22) | collective-permute-done | bytes 524320 | tf_op jit(solution)/shard_map/ppermute | solution.py:19
  166.7 5.7 %collective-permute-start.23 = (bf16[2,1024,256]{2,1,0:T(8,128)(2,1)S(1)}, bf16[2,1024,256]{2,1,0:T(8,128)(2,1)S(1)}, u32[]{:S(2)}, u32[]{:S(2)}) collective-permute-start(bf16[2,1024,256]{2,1,0:T(8,128)(2,1)S(1)} %maximum_select_fusion.2), channel_id=1, source_target_pairs={{0,16},{16,0},{32,48},{48,32},{64,80},{80,64},{96,112},{112,96},{1... | collective-permute-start | bytes 3145736 | tf_op jit(solution)/shard_map/ppermute | solution.py:19
  175.2 3.0 fusion.15
  185.2 10.5 %convolution_select_fusion = f32[8,136,32]{2,0,1:T(8,128)} fusion(bf16[32,64,256]{2,1,0:T(8,128)(2,1)S(1)} %bitcast.126, bf16[256,1,7,63]{0,2,3,1:T(8,128)(2,1)S(1)} %slice.125, bf16[256,1,8,136]{0,2,3,1:T(8,128)(2,1)S(1)} %copy.61, pred[8,136]{0,1:T(8,128)(4,1)S(1)} %copy-done.22), kind=kOutput, calls=%fused_computation.23 | convolution fusion | flops 1143330816 | bytes 1971776 | tf_op jit(solution)/shard_map/conv_general_dilated | solution.py:95
  197.2 3.4 %collective-permute-start.25 = (f32[32,1024]{1,0:T(8,128)S(1)}, f32[32,1024]{1,0:T(8,128)S(1)}, u32[]{:S(2)}, u32[]{:S(2)}) collective-permute-start(f32[32,1024]{1,0:T(8,128)S(1)} %slice_bitcast_fusion.4), channel_id=1, source_target_pairs={{0,2},{2,0},{4,6},{6,4},{8,10},{10,8},{12,14},{14,12},{1,3},{3,1},... | collective-permute-start | bytes 393224 | tf_op jit(solution)/shard_map/ppermute | solution.py:19
  203.2 4.7 %collective-permute-done.26 = f32[32,1024]{1,0:T(8,128)S(1)} collective-permute-done((f32[32,1024]{1,0:T(8,128)S(1)}, f32[32,1024]{1,0:T(8,128)S(1)}, u32[]{:S(2)}, u32[]{:S(2)}) %collective-permute-start.26) | collective-permute-done | bytes 131104 | tf_op jit(solution)/shard_map/ppermute | solution.py:19
  208.7 3.4 %collective-permute-start.28 = (f32[32,64]{1,0:T(8,128)S(1)}, f32[32,64]{1,0:T(8,128)S(1)}, u32[]{:S(2)}, u32[]{:S(2)}) collective-permute-start(f32[32,64]{1,0:T(8,128)S(1)} %reduce_sum.22), channel_id=1, source_target_pairs={{0,2},{2,0},{4,6},{6,4},{8,10},{10,8},{12,14},{14,12},{1,3},{3,1},... | collective-permute-start | bytes 24584 | tf_op jit(solution)/shard_map/ppermute | solution.py:19
  222.1 6.9 %collective-permute-start.31 = (bf16[32,63]{1,0:T(8,128)(2,1)S(1)}, bf16[32,63]{1,0:T(8,128)(2,1)S(1)}, u32[]{:S(2)}, u32[]{:S(2)}) collective-permute-start(bf16[32,63]{1,0:T(8,128)(2,1)S(1)} %slice.128), channel_id=1, source_target_pairs={{0,16},{16,32},{32,48},{48,64},{64,80},{80,96},{96,112},{1,17},{17... | collective-permute-start | bytes 12104 | tf_op jit(solution)/shard_map/ppermute | solution.py:14
  236.9 4.0 %fusion.21 = f32[8,136,256]{2,0,1:T(8,128)S(1)} fusion(bf16[64,64,256]{2,1,0:T(8,128)(2,1)S(1)} %bitcast.114, pred[8,136]{0,1:T(8,128)(4,1)} %constant.149, bf16[64,1,7,63]{0,2,3,1:T(8,128)(2,1)S(1)} %slice.129, bf16[64,1,8,136]{0,2,3,1:T(8,128)(2,1)} %copy.65), kind=kOutput, calls=%fused_computation.22 | convolution fusion | flops 2282869760 | bytes 3408064 | tf_op jit(solution)/shard_map/conv_general_dilated | solution.py:87
  241.9 14.6 %fusion.33 = f32[32,64,256]{2,0,1:T(8,128)S(1)} fusion(bf16[1,32,1087]{1,0,2:T(2,128)(2,1)S(1)} %copy-done.6, bf16[1,256,1024]{1,2,0:T(8,128)(2,1)S(1)} %fusion.54), kind=kOutput, calls=%fused_computation.42 | convolution fusion | flops 1073741824 | bytes 2691008 | tf_op jit(solution)/shard_map/conv_general_dilated | solution.py:103
  264.5 11.9 %collective-permute-done.35 = f32[512,256]{1,0:T(8,128)S(1)} collective-permute-done((f32[512,256]{1,0:T(8,128)S(1)}, f32[512,256]{1,0:T(8,128)S(1)}, u32[]{:S(2)}, u32[]{:S(2)}) %collective-permute-start.35) | collective-permute-done | bytes 524320 | tf_op jit(solution)/shard_map/ppermute | solution.py:19
  291.0 4.2 %collective-permute-done.40 = f32[256,256]{1,0:T(8,128)S(1)} collective-permute-done((f32[256,256]{1,0:T(8,128)S(1)}, f32[256,256]{1,0:T(8,128)S(1)}, u32[]{:S(2)}, u32[]{:S(2)}) %collective-permute-start.40) | collective-permute-done | bytes 262176 | tf_op jit(solution)/shard_map/ppermute | solution.py:19
  296.6 8.3 %collective-permute-done.41 = f32[512,256]{1,0:T(8,128)S(1)} collective-permute-done((f32[512,256]{1,0:T(8,128)S(1)}, f32[512,256]{1,0:T(8,128)S(1)}, u32[]{:S(2)}, u32[]{:S(2)}) %collective-permute-start.41) | collective-permute-done | bytes 524320 | tf_op jit(solution)/shard_map/ppermute | solution.py:19
  305.0 4.9 %collective-permute-start.42 = (f32[1024,256]{1,0:T(8,128)S(1)}, f32[1024,256]{1,0:T(8,128)S(1)}, u32[]{:S(2)}, u32[]{:S(2)}) collective-permute-start(f32[1024,256]{1,0:T(8,128)S(1)} %maximum_select_fusion.3), channel_id=1, source_target_pairs={{0,16},{16,0},{32,48},{48,32},{64,80},{80,64},{96,112},{112,96},{1... | collective-permute-start | bytes 3145736 | tf_op jit(solution)/shard_map/ppermute | solution.py:19
  (215 shorter events, 109.1 us)
Async XLA Ops:
  3.6 28.5 %collective-permute-start.3 = (bf16[32,64,256]{2,0,1:T(8,128)(2,1)S(1)}, bf16[32,64,256]{2,0,1:T(8,128)(2,1)}, u32[]{:S(2)}, u32[]{:S(2)}) collective-permute-start(bf16[32,64,256]{2,0,1:T(8,128)(2,1)S(1)} %get-tuple-element.5), channel_id=1, source_target_pairs={{0,1},{1,0},{2,3},{3,2},{4,5},{5,4},{6,7},{7,6},{8,9},{9,8},{10,11... | collective-permute-start | bytes 3145736 | tf_op jit(solution)/shard_map/ppermute | solution.py:19
  6.2 25.1 %collective-permute-start.2 = (bf16[32,1024]{1,0:T(8,128)(2,1)S(1)}, bf16[32,1024]{1,0:T(8,128)(2,1)S(1)}, u32[]{:S(2)}, u32[]{:S(2)}) collective-permute-start(bf16[32,1024]{1,0:T(8,128)(2,1)S(1)} %convert_element_type.40), channel_id=1, source_target_pairs={{0,1},{1,0},{2,3},{3,2},{4,5},{5,4},{6,7},{7,6},{8,9},{9,8},{10,11... | collective-permute-start | bytes 196616 | tf_op jit(solution)/shard_map/ppermute | solution.py:19
  6.4 24.9 %collective-permute-start.1 = (bf16[32,63]{1,0:T(8,128)(2,1)S(1)}, bf16[32,63]{1,0:T(8,128)(2,1)S(1)}, u32[]{:S(2)}, u32[]{:S(2)}) collective-permute-start(bf16[32,63]{1,0:T(8,128)(2,1)S(1)} %slice.108), channel_id=1, source_target_pairs={{0,17},{1,16},{16,33},{17,32},{32,49},{33,48},{48,65},{49,64},{64,... | collective-permute-start | bytes 12104 | tf_op jit(solution)/shard_map/ppermute | solution.py:78
  11.8 19.5 %collective-permute-start = (bf16[32,63]{1,0:T(8,128)(2,1)S(1)}, bf16[32,63]{1,0:T(8,128)(2,1)S(1)}, u32[]{:S(2)}, u32[]{:S(2)}) collective-permute-start(bf16[32,63]{1,0:T(8,128)(2,1)S(1)} %slice.108), channel_id=1, source_target_pairs={{0,16},{16,32},{32,48},{48,64},{64,80},{80,96},{96,112},{1,17},{17... | collective-permute-start | bytes 12104 | tf_op jit(solution)/shard_map/ppermute | solution.py:14
  36.5 5.2 %collective-permute-start.4 = (bf16[256,63]{0,1:T(8,128)(2,1)S(1)}, bf16[256,63]{0,1:T(8,128)(2,1)S(1)}, u32[]{:S(2)}, u32[]{:S(2)}) collective-permute-start(bf16[256,63]{0,1:T(8,128)(2,1)S(1)} %slice.111), channel_id=1, source_target_pairs={{16,0},{32,16},{48,32},{64,48},{80,64},{96,80},{112,96},{17,1},{33... | collective-permute-start | bytes 96776 | tf_op jit(solution)/shard_map/ppermute | solution.py:14
  51.9 5.9 %collective-permute-start.5 = (f32[32,1024]{1,0:T(8,128)S(1)}, f32[32,1024]{1,0:T(8,128)S(1)}, u32[]{:S(2)}, u32[]{:S(2)}) collective-permute-start(f32[32,1024]{1,0:T(8,128)S(1)} %slice_bitcast_fusion.5), channel_id=1, source_target_pairs={{0,2},{2,0},{4,6},{6,4},{8,10},{10,8},{12,14},{14,12},{1,3},{3,1},... | collective-permute-start | bytes 393224 | tf_op jit(solution)/shard_map/ppermute | solution.py:19
  57.8 4.9 %collective-permute-start.6 = (f32[32,1024]{1,0:T(8,128)S(1)}, f32[32,1024]{1,0:T(8,128)S(1)}, u32[]{:S(2)}, u32[]{:S(2)}) collective-permute-start(f32[32,1024]{1,0:T(8,128)S(1)} %fusion.119), channel_id=1, source_target_pairs={{0,4},{2,6},{4,0},{6,2},{8,12},{10,14},{12,8},{14,10},{1,5},{3,7},... | collective-permute-start | bytes 393224 | tf_op jit(solution)/shard_map/ppermute | solution.py:19
  62.7 14.7 %collective-permute-start.7 = (f32[32,1024]{1,0:T(8,128)S(1)}, f32[32,1024]{1,0:T(8,128)S(1)}, u32[]{:S(2)}, u32[]{:S(2)}) collective-permute-start(f32[32,1024]{1,0:T(8,128)S(1)} %add.147), channel_id=1, source_target_pairs={{0,8},{2,10},{4,12},{6,14},{8,0},{10,2},{12,4},{14,6},{1,9},{3,11}... | collective-permute-start | bytes 393224 | tf_op jit(solution)/shard_map/ppermute | solution.py:19
  65.5 4.8 %collective-permute-start.8 = (f32[32,64]{0,1:T(8,128)S(1)}, f32[32,64]{0,1:T(8,128)S(1)}, u32[]{:S(2)}, u32[]{:S(2)}) collective-permute-start(f32[32,64]{0,1:T(8,128)S(1)} %get-tuple-element.4), channel_id=1, source_target_pairs={{0,2},{2,0},{4,6},{6,4},{8,10},{10,8},{12,14},{14,12},{1,3},{3,1},... | collective-permute-start | bytes 24584 | tf_op jit(solution)/shard_map/ppermute | solution.py:19
  73.1 4.3 %collective-permute-start.10 = (f32[32,64]{0,1:T(8,128)S(1)}, f32[32,64]{0,1:T(8,128)S(1)}, u32[]{:S(2)}, u32[]{:S(2)}) collective-permute-start(f32[32,64]{0,1:T(8,128)S(1)} %add.150), channel_id=1, source_target_pairs={{0,8},{2,10},{4,12},{6,14},{8,0},{10,2},{12,4},{14,6},{1,9},{3,11}... | collective-permute-start | bytes 24584 | tf_op jit(solution)/shard_map/ppermute | solution.py:19
  78.4 11.1 %collective-permute-start.11 = (bf16[32,63]{1,0:T(8,128)(2,1)S(1)}, bf16[32,63]{1,0:T(8,128)(2,1)S(1)}, u32[]{:S(2)}, u32[]{:S(2)}) collective-permute-start(bf16[32,63]{1,0:T(8,128)(2,1)S(1)} %slice.114), channel_id=1, source_target_pairs={{0,16},{16,32},{32,48},{48,64},{64,80},{80,96},{96,112},{1,17},{17... | collective-permute-start | bytes 12104 | tf_op jit(solution)/shard_map/ppermute | solution.py:14
  86.2 5.0 %collective-permute-start.12 = (bf16[32,63]{1,0:T(8,128)(2,1)S(1)}, bf16[32,63]{1,0:T(8,128)(2,1)S(1)}, u32[]{:S(2)}, u32[]{:S(2)}) collective-permute-start(bf16[32,63]{1,0:T(8,128)(2,1)S(1)} %slice.114), channel_id=1, source_target_pairs={{0,17},{1,16},{16,33},{17,32},{32,49},{33,48},{48,65},{49,64},{64,... | collective-permute-start | bytes 12104 | tf_op jit(solution)/shard_map/ppermute | solution.py:78
  113.2 4.2 %collective-permute-start.14 = (f32[1024,256]{1,0:T(8,128)S(1)}, f32[1024,256]{1,0:T(8,128)S(1)}, u32[]{:S(2)}, u32[]{:S(2)}) collective-permute-start(f32[1024,256]{1,0:T(8,128)S(1)} %bitcast.125), channel_id=1, source_target_pairs={{0,16},{16,0},{32,48},{48,32},{64,80},{80,64},{96,112},{112,96},{1... | collective-permute-start | bytes 3145736 | tf_op jit(solution)/shard_map/ppermute | solution.py:19
  117.6 13.2 %collective-permute-start.15 = (f32[512,256]{1,0:T(8,128)S(1)}, f32[512,256]{1,0:T(8,128)S(1)}, u32[]{:S(2)}, u32[]{:S(2)}) collective-permute-start(f32[512,256]{1,0:T(8,128)S(1)} %slice_select_fusion.1), channel_id=1, source_target_pairs={{0,32},{16,48},{32,0},{48,16},{64,96},{80,112},{96,64},{112,80},{1... | collective-permute-start | bytes 1572872 | tf_op jit(solution)/shard_map/ppermute | solution.py:19
  130.9 11.5 %collective-permute-start.16 = (f32[256,256]{1,0:T(8,128)S(1)}, f32[256,256]{1,0:T(8,128)S(1)}, u32[]{:S(2)}, u32[]{:S(2)}) collective-permute-start(f32[256,256]{1,0:T(8,128)S(1)} %slice_select_fusion.3), channel_id=1, source_target_pairs={{0,64},{16,80},{32,96},{48,112},{64,0},{80,16},{96,32},{112,48},{1... | collective-permute-start | bytes 786440 | tf_op jit(solution)/shard_map/ppermute | solution.py:19
  138.1 4.3 %collective-permute-start.19 = (f32[2048]{0:T(1024)S(1)}, f32[2048]{0:T(1024)S(1)}, u32[]{:S(2)}, u32[]{:S(2)}) collective-permute-start(f32[2048]{0:T(1024)S(1)} %add.163), channel_id=1, source_target_pairs={{0,64},{16,80},{32,96},{48,112},{64,0},{80,16},{96,32},{112,48},{1... | collective-permute-start | bytes 24584 | tf_op jit(solution)/shard_map/ppermute | solution.py:19
  148.1 6.8 %collective-permute-start.21 = (bf16[2,256,256]{2,1,0:T(8,128)(2,1)S(1)}, bf16[2,256,256]{2,1,0:T(8,128)(2,1)S(1)}, u32[]{:S(2)}, u32[]{:S(2)}) collective-permute-start(bf16[2,256,256]{2,1,0:T(8,128)(2,1)S(1)} %pad_maximum_fusion.11), channel_id=1, source_target_pairs={{0,64},{16,80},{32,96},{48,112},{64,0},{80,16},{96,32},{112,48},{1... | collective-permute-start | bytes 786440 | tf_op jit(solution)/shard_map/ppermute | solution.py:19
  155.1 11.2 %collective-permute-start.22 = (bf16[2,512,256]{2,1,0:T(8,128)(2,1)S(1)}, bf16[2,512,256]{2,1,0:T(8,128)(2,1)S(1)}, u32[]{:S(2)}, u32[]{:S(2)}) collective-permute-start(bf16[2,512,256]{2,1,0:T(8,128)(2,1)S(1)} %maximum_select_fusion.4), channel_id=1, source_target_pairs={{0,32},{16,48},{32,0},{48,16},{64,96},{80,112},{96,64},{112,80},{1... | collective-permute-start | bytes 1572872 | tf_op jit(solution)/shard_map/ppermute | solution.py:19
  166.7 8.0 %collective-permute-start.23 = (bf16[2,1024,256]{2,1,0:T(8,128)(2,1)S(1)}, bf16[2,1024,256]{2,1,0:T(8,128)(2,1)S(1)}, u32[]{:S(2)}, u32[]{:S(2)}) collective-permute-start(bf16[2,1024,256]{2,1,0:T(8,128)(2,1)S(1)} %maximum_select_fusion.2), channel_id=1, source_target_pairs={{0,16},{16,0},{32,48},{48,32},{64,80},{80,64},{96,112},{112,96},{1... | collective-permute-start | bytes 3145736 | tf_op jit(solution)/shard_map/ppermute | solution.py:19
  179.7 5.2 %collective-permute-start.24 = (bf16[256,63]{0,1:T(8,128)(2,1)S(1)}, bf16[256,63]{0,1:T(8,128)(2,1)S(1)}, u32[]{:S(2)}, u32[]{:S(2)}) collective-permute-start(bf16[256,63]{0,1:T(8,128)(2,1)S(1)} %slice.124), channel_id=1, source_target_pairs={{16,0},{32,16},{48,32},{64,48},{80,64},{96,80},{112,96},{17,1},{33... | collective-permute-start | bytes 96776 | tf_op jit(solution)/shard_map/ppermute | solution.py:14
  197.2 5.8 %collective-permute-start.25 = (f32[32,1024]{1,0:T(8,128)S(1)}, f32[32,1024]{1,0:T(8,128)S(1)}, u32[]{:S(2)}, u32[]{:S(2)}) collective-permute-start(f32[32,1024]{1,0:T(8,128)S(1)} %slice_bitcast_fusion.4), channel_id=1, source_target_pairs={{0,2},{2,0},{4,6},{6,4},{8,10},{10,8},{12,14},{14,12},{1,3},{3,1},... | collective-permute-start | bytes 393224 | tf_op jit(solution)/shard_map/ppermute | solution.py:19
  203.0 4.9 %collective-permute-start.26 = (f32[32,1024]{1,0:T(8,128)S(1)}, f32[32,1024]{1,0:T(8,128)S(1)}, u32[]{:S(2)}, u32[]{:S(2)}) collective-permute-start(f32[32,1024]{1,0:T(8,128)S(1)} %fusion.120), channel_id=1, source_target_pairs={{0,4},{2,6},{4,0},{6,2},{8,12},{10,14},{12,8},{14,10},{1,5},{3,7},... | collective-permute-start | bytes 393224 | tf_op jit(solution)/shard_map/ppermute | solution.py:19
  207.9 12.3 %collective-permute-start.27 = (f32[32,1024]{1,0:T(8,128)S(1)}, f32[32,1024]{1,0:T(8,128)}, u32[]{:S(2)}, u32[]{:S(2)}) collective-permute-start(f32[32,1024]{1,0:T(8,128)S(1)} %add.166), channel_id=1, source_target_pairs={{0,8},{2,10},{4,12},{6,14},{8,0},{10,2},{12,4},{14,6},{1,9},{3,11}... | collective-permute-start | bytes 393224 | tf_op jit(solution)/shard_map/ppermute | solution.py:19
  208.7 4.9 %collective-permute-start.28 = (f32[32,64]{1,0:T(8,128)S(1)}, f32[32,64]{1,0:T(8,128)S(1)}, u32[]{:S(2)}, u32[]{:S(2)}) collective-permute-start(f32[32,64]{1,0:T(8,128)S(1)} %reduce_sum.22), channel_id=1, source_target_pairs={{0,2},{2,0},{4,6},{6,4},{8,10},{10,8},{12,14},{14,12},{1,3},{3,1},... | collective-permute-start | bytes 24584 | tf_op jit(solution)/shard_map/ppermute | solution.py:19
  216.2 4.1 %collective-permute-start.30 = (f32[32,64]{1,0:T(8,128)S(1)}, f32[32,64]{1,0:T(8,128)S(1)}, u32[]{:S(2)}, u32[]{:S(2)}) collective-permute-start(f32[32,64]{1,0:T(8,128)S(1)} %add.169), channel_id=1, source_target_pairs={{0,8},{2,10},{4,12},{6,14},{8,0},{10,2},{12,4},{14,6},{1,9},{3,11}... | collective-permute-start | bytes 24584 | tf_op jit(solution)/shard_map/ppermute | solution.py:19
  222.1 10.3 %collective-permute-start.31 = (bf16[32,63]{1,0:T(8,128)(2,1)S(1)}, bf16[32,63]{1,0:T(8,128)(2,1)S(1)}, u32[]{:S(2)}, u32[]{:S(2)}) collective-permute-start(bf16[32,63]{1,0:T(8,128)(2,1)S(1)} %slice.128), channel_id=1, source_target_pairs={{0,16},{16,32},{32,48},{48,64},{64,80},{80,96},{96,112},{1,17},{17... | collective-permute-start | bytes 12104 | tf_op jit(solution)/shard_map/ppermute | solution.py:14
  229.0 5.1 %collective-permute-start.32 = (bf16[32,63]{1,0:T(8,128)(2,1)S(1)}, bf16[32,63]{1,0:T(8,128)(2,1)S(1)}, u32[]{:S(2)}, u32[]{:S(2)}) collective-permute-start(bf16[32,63]{1,0:T(8,128)(2,1)S(1)} %slice.128), channel_id=1, source_target_pairs={{0,17},{1,16},{16,33},{17,32},{32,49},{33,48},{48,65},{49,64},{64,... | collective-permute-start | bytes 12104 | tf_op jit(solution)/shard_map/ppermute | solution.py:78
  261.7 14.8 %collective-permute-start.35 = (f32[512,256]{1,0:T(8,128)S(1)}, f32[512,256]{1,0:T(8,128)S(1)}, u32[]{:S(2)}, u32[]{:S(2)}) collective-permute-start(f32[512,256]{1,0:T(8,128)S(1)} %slice_select_fusion), channel_id=1, source_target_pairs={{0,32},{16,48},{32,0},{48,16},{64,96},{80,112},{96,64},{112,80},{1... | collective-permute-start | bytes 1572872 | tf_op jit(solution)/shard_map/ppermute | solution.py:19
  276.6 11.8 %collective-permute-start.36 = (f32[256,256]{1,0:T(8,128)S(1)}, f32[256,256]{1,0:T(8,128)S(1)}, u32[]{:S(2)}, u32[]{:S(2)}) collective-permute-start(f32[256,256]{1,0:T(8,128)S(1)} %slice_select_fusion.2), channel_id=1, source_target_pairs={{0,64},{16,80},{32,96},{48,112},{64,0},{80,16},{96,32},{112,48},{1... | collective-permute-start | bytes 786440 | tf_op jit(solution)/shard_map/ppermute | solution.py:19
  288.5 6.8 %collective-permute-start.40 = (f32[256,256]{1,0:T(8,128)S(1)}, f32[256,256]{1,0:T(8,128)S(1)}, u32[]{:S(2)}, u32[]{:S(2)}) collective-permute-start(f32[256,256]{1,0:T(8,128)S(1)} %multiply_divide_fusion), channel_id=1, source_target_pairs={{0,64},{16,80},{32,96},{48,112},{64,0},{80,16},{96,32},{112,48},{1... | collective-permute-start | bytes 786440 | tf_op jit(solution)/shard_map/ppermute | solution.py:19
  295.3 9.6 %collective-permute-start.41 = (f32[512,256]{1,0:T(8,128)S(1)}, f32[512,256]{1,0:T(8,128)S(1)}, u32[]{:S(2)}, u32[]{:S(2)}) collective-permute-start(f32[512,256]{1,0:T(8,128)S(1)} %maximum_select_fusion.5), channel_id=1, source_target_pairs={{0,32},{16,48},{32,0},{48,16},{64,96},{80,112},{96,64},{112,80},{1... | collective-permute-start | bytes 1572872 | tf_op jit(solution)/shard_map/ppermute | solution.py:19
  305.0 7.2 %collective-permute-start.42 = (f32[1024,256]{1,0:T(8,128)S(1)}, f32[1024,256]{1,0:T(8,128)S(1)}, u32[]{:S(2)}, u32[]{:S(2)}) collective-permute-start(f32[1024,256]{1,0:T(8,128)S(1)} %maximum_select_fusion.3), channel_id=1, source_target_pairs={{0,16},{16,0},{32,48},{48,32},{64,80},{80,64},{96,112},{112,96},{1... | collective-permute-start | bytes 3145736 | tf_op jit(solution)/shard_map/ppermute | solution.py:19
  (38 other events, 447.9 us)

commit v4 on v3

--- a/solution.py
+++ b/solution.py
@@ -78,6 +78,25 @@
     return lax.ppermute(value, ("tm", "motif"), pairs)
 
 
+def spread_sum(value, axis):
+    count = lax.axis_size(axis)
+    parts = value.reshape(count, value.shape[0] // count, *value.shape[1:])
+    return jnp.sum(lax.all_to_all(parts, axis, 0, 0, tiled=True), axis=0)
+
+
+def spread_gather(value, axis):
+    count = lax.axis_size(axis)
+    copies = jnp.broadcast_to(value[None], (count, *value.shape))
+    gathered = lax.all_to_all(copies, axis, 0, 0, tiled=True)
+    return gathered.reshape(count * value.shape[0], *value.shape[1:])
+
+
+def full_sum(value, axis):
+    count = lax.axis_size(axis)
+    copies = jnp.broadcast_to(value[None], (count, *value.shape))
+    return jnp.sum(lax.all_to_all(copies, axis, 0, 0, tiled=True), axis=0)
+
+
 CONV_DIMS = lax.ConvDimensionNumbers
 
 
@@ -120,8 +139,8 @@
     weight_bfloat = motif_w.astype(jnp.bfloat16)
     weight_all = jnp.concatenate([weight_bfloat, xor_swap(weight_bfloat, "motif", 1)], axis=0)
     acts = motif_h
-    offset = scatter_offset("tm", rows)
     part_rows = rows // lax.axis_size("tm")
+    offset = lax.axis_index("tm") * part_rows
     weight_part = lax.dynamic_slice_in_dim(weights, offset, part_rows, axis=0)
     place = jnp.arange(width + rim, dtype=jnp.int32)[:, None]
     lag_ids = jnp.arange(lags, dtype=jnp.int32)[None, :]
@@ -150,24 +169,24 @@
         rext = jnp.concatenate([ratio, after], axis=1)
         hnum = hnum_of(weight_bfloat, rext)
         colsum = jnp.sum(weight_bfloat, axis=2, dtype=jnp.float32)
-        hnum, colsum = all_sum((hnum, colsum), "neuron")
+        joined = full_sum(jnp.concatenate([hnum, colsum], axis=1), "neuron")
+        hnum, colsum = joined[:, :width], joined[:, width:]
         hden = jnp.dot(colsum, mask, precision=lax.Precision.HIGHEST)
         acts = acts * hnum / hden
         hext, hext_all = extend_padded(acts)
         ratio = ratio_of(weight_all, hext_all)
         wnum = wnum_of(hext, ratio).reshape(rows, n_dev)
         wden = jnp.dot(hext, window, preferred_element_type=jnp.float32).reshape(rows)
-        wnum = sum_scatter(wnum, "tm")
-        wden = all_sum(wden, "tm")
-        wden_part = lax.dynamic_slice_in_dim(wden, offset, part_rows, axis=0)
+        wnum = spread_sum(wnum, "tm")
+        wden_part = spread_sum(wden, "tm")
         weight_part = weight_part * wnum / wden_part[:, None]
         if step + 1 < ITERS:
             part_bfloat = weight_part.astype(jnp.bfloat16)
             pair = jnp.stack([part_bfloat, xor_swap(part_bfloat, "motif", 1)], axis=0)
-            pair = gather_rows(pair, "tm", dim=1)
-            weight_all = pair.reshape(2 * k_dev, lags, n_dev)
+            pair = spread_gather(jnp.swapaxes(pair, 0, 1), "tm")
+            weight_all = jnp.swapaxes(pair, 0, 1).reshape(2 * k_dev, lags, n_dev)
             weight_bfloat = weight_all[:k_dev]
-    weights = gather_rows(weight_part, "tm")
+    weights = spread_gather(weight_part, "tm")
     return (weights.reshape(k_dev, lags, n_dev), acts)
 
 

time: 319 us -> 350 us (1.097)
  blocking collectives: 0 us -> 82.9 us
  starting transfers between devices: 98.1 us -> 56.4 us
  waiting for transfers between devices: 121 us -> 90.4 us
  local copies, waits for them, and re-layouts: 15.4 us -> 30.4 us
  matrix products: 66.8 us -> 70.3 us
    ppermute x35 -> x5, waiting for transfers between devices: 98.4 us -> 3.13 us  [xor_swap(): lax.ppermute(value, axis, [(source, source ^ mask) for source in range(co...]
    all_to_all x0 -> x3, blocking collectives: none -> 82.9 us  [the longest x2 60.3 us: spread_gather(): gathered = lax.all_to_all(copies, axis, 0, 0, tiled=True)]
    all_to_all x0 -> x5, waiting for transfers between devices: none -> 67.4 us  [the longest x4 50.9 us: spread_sum(): return jnp.sum(lax.all_to_all(parts, axis, 0, 0, tiled=True), axis=0)]
    ppermute x35 -> x5, starting transfers between devices: 66.1 us -> 5.1 us  [xor_swap(): lax.ppermute(value, axis, [(source, source ^ mask) for source in range(co...]
    all_to_all x0 -> x5, starting transfers between devices: none -> 25.8 us  [the longest x4 18.7 us: spread_sum(): return jnp.sum(lax.all_to_all(parts, axis, 0, 0, tiled=True), axis=0)]
    rev x0 -> x4, local copies, waits for them, and re-layouts: none -> 8.53 us  [wnum_of(): return jnp.flip(out, axis=1)]
    ppermute x5, starting transfers between devices: 21.8 us -> 15 us  [from_behind(): lax.ppermute(value, axis, [(source, source + steps) for source in range(f...]
    unnamed x55 -> x48, local copies, waits for them, and re-layouts: 1.79 us -> 6.53 us
  transfers between devices with their start and end apart: 43 -> 18, of which waited for: 34 -> 6; matrix products, arithmetic and copies ran while one was open for 2% -> 18% of each run, Pallas kernels for 0% -> 0%
where the time goes in v4:
time: 350 us; the launch traced here: 345 us
  waiting for transfers between devices  90.4 us (26%)
  blocking collectives  82.9 us (24%)
  matrix products  70.3 us (20%)
  starting transfers between devices  56.4 us (16%)
  local copies, waits for them, and re-layouts  30.4 us (9%)
  other arithmetic  12.4 us (4%)
    all_to_all x2, blocking collectives, spread_gather(): gathered = lax.all_to_all(copies, axis, 0, 0, tiled=True)  60.3 us
    all_to_all x4, waiting for transfers between devices, spread_sum(): return jnp.sum(lax.all_to_all(parts, axis, 0, 0, tiled=True), axis=0)  50.9 us
    conv_general_dilated x2, matrix products, wnum_of(): lax.conv_general_dilated(hext[None], ratio[None], (1,), [(0, 0)], dimensi...  32 us
    all_to_all x1, blocking collectives, full_sum(): return jnp.sum(lax.all_to_all(copies, axis, 0, 0, tiled=True), axis=0)  22.6 us
    conv_general_dilated x2, matrix products, hnum_of(): lax.conv_general_dilated(rext[None], weight_bfloat, (1,), [(0, 0)], dimen...  19.8 us
    all_to_all x4, starting transfers between devices, spread_sum(): return jnp.sum(lax.all_to_all(parts, axis, 0, 0, tiled=True), axis=0)  18.7 us
    ppermute x3, waiting for transfers between devices, from_behind_other(): return lax.ppermute(value, ('tm', 'motif'), pairs)  17.2 us
    all_to_all x1, waiting for transfers between devices, full_sum(): return jnp.sum(lax.all_to_all(copies, axis, 0, 0, tiled=True), axis=0)  16.5 us
  transfers between devices with their start and end apart: 18, of which 6 were waited for; matrix products, arithmetic and copies ran while one was open for 18% of the time, Pallas kernels for 0%

profile of v4, /device:TPU:1, one launch (start us, length us, event | category | flops | bytes accessed | tf_op | source)
XLA Modules:
  0.0 344.7 jit_solution(2844051844069504490)
XLA Ops:
  0.6 3.0 convert_reduce_fusion.1
  3.6 2.5 collective-permute-start.3
  6.3 5.5 %collective-permute-start.1 = (bf16[32,63]{1,0:T(8,128)(2,1)S(1)}, bf16[32,63]{1,0:T(8,128)(2,1)S(1)}, u32[]{:S(2)}, u32[]{:S(2)}) collective-permute-start(bf16[32,63]{1,0:T(8,128)(2,1)S(1)} %slice.56), channel_id=1, source_target_pairs={{0,17},{1,16},{16,33},{17,32},{32,49},{33,48},{48,65},{49,64},{64,... | collective-permute-start | bytes 12104 | tf_op jit(solution)/shard_map/ppermute | solution.py:78
  14.1 17.2 %collective-permute-done.1 = bf16[32,63]{1,0:T(8,128)(2,1)S(1)} collective-permute-done((bf16[32,63]{1,0:T(8,128)(2,1)S(1)}, bf16[32,63]{1,0:T(8,128)(2,1)S(1)}, u32[]{:S(2)}, u32[]{:S(2)}) %collective-permute-start.1) | collective-permute-done | bytes 4064 | tf_op jit(solution)/shard_map/ppermute | solution.py:78
  32.1 3.8 %fusion.9 = f32[8,136,256]{2,0,1:T(8,128)S(1)} fusion(bf16[32,64,256]{2,0,1:T(8,128)(2,1)} %collective-permute-done.3, bf16[32,64,256]{2,0,1:T(8,128)(2,1)S(1)} %get-tuple-element.3, pred[8,136]{0,1:T(8,128)(4,1)} %constant.49, bf16[64,1,7,63]{0,2,3,1:T(8,128)(2,1)S(1)} %slice.57, bf16[64,1,8,136]{0,2,3,1:T(8,128)(2,1)S(1)} %copy.77), kind=kOutput, calls=%fused_computation.14 | convolution fusion | flops 2287064064 | bytes 3408064 | tf_op jit(solution)/shard_map/conv_general_dilated | solution.py:106
  36.5 2.5 collective-permute-start.4
  39.0 2.7 collective-permute-done.4
  42.5 9.3 %convolution_select_fusion.1 = f32[8,136,32]{2,0,1:T(8,128)S(1)} fusion(bf16[32,64,256]{2,0,1:T(8,128)(2,1)S(1)} %get-tuple-element.3, bf16[256,1,7,63]{0,2,3,1:T(8,128)(2,1)S(1)} %slice.60, bf16[256,1,8,136]{0,2,3,1:T(8,128)(2,1)S(1)} %copy.81, pred[8,136]{0,1:T(8,128)(4,1)S(1)} %copy-done.16), kind=kOutput, calls=%fused_computation.22 | convolution fusion | flops 1143330816 | bytes 1971776 | tf_op jit(solution)/shard_map/conv_general_dilated | solution.py:114
  53.5 7.2 %all-to-all-start = ((f32[8,32,1088]{2,1,0:T(8,128)}), f32[8,32,1088]{2,1,0:T(8,128)S(1)}, u32[]{:S(2)}, u32[]{:S(2)}) async-start(f32[8,32,1088]{2,1,0:T(8,128)} %broadcast_in_dim.28), calls=%async_computation | async-start | bytes 2359296 | tf_op jit(solution)/shard_map/all_to_all | solution.py:97
  61.2 16.5 %all-to-all-done = f32[8,32,1088]{2,1,0:T(8,128)S(1)} async-done(((f32[8,32,1088]{2,1,0:T(8,128)}), f32[8,32,1088]{2,1,0:T(8,128)S(1)}, u32[]{:S(2)}, u32[]{:S(2)}) %all-to-all-start) | async-done | bytes 1114144 | tf_op jit(solution)/shard_map/all_to_all | solution.py:97
  79.4 4.5 %collective-permute-start.5 = (bf16[32,63]{1,0:T(8,128)(2,1)S(1)}, bf16[32,63]{1,0:T(8,128)(2,1)S(1)}, u32[]{:S(2)}, u32[]{:S(2)}) collective-permute-start(bf16[32,63]{1,0:T(8,128)(2,1)S(1)} %slice.64), channel_id=1, source_target_pairs={{0,16},{16,32},{32,48},{48,64},{64,80},{80,96},{96,112},{1,17},{17... | collective-permute-start | bytes 12104 | tf_op jit(solution)/shard_map/ppermute | solution.py:14
  84.0 2.7 collective-permute-start.6
  88.5 4.3 %all-to-all-start.2 = ((f32[8,1,256]{2,1,0:T(1,128)}), f32[8,1,256]{2,1,0:T(1,128)}, u32[]{:S(2)}, u32[]{:S(2)}) async-start(f32[8,1,256]{2,1,0:T(1,128)} %all_to_all.40), calls=%async_computation.2 | async-start | bytes 16384 | tf_op jit(solution)/shard_map/all_to_all | solution.py:84
  94.9 3.8 %fusion.11 = f32[8,136,256]{2,0,1:T(8,128)S(1)} fusion(bf16[32,64,256]{2,0,1:T(8,128)(2,1)} %collective-permute-done.3, bf16[32,64,256]{2,0,1:T(8,128)(2,1)S(1)} %get-tuple-element.3, pred[8,136]{0,1:T(8,128)(4,1)S(1)} %copy-done.17, bf16[64,1,7,63]{0,2,3,1:T(8,128)(2,1)S(1)} %slice.65, bf16[64,1,8,136]{0,2,3,1:T(8,128)(2,1)S(1)} %copy.85), kind=kOutput, calls=%fused_computation.16 | convolution fusion | flops 2287064064 | bytes 3408064 | tf_op jit(solution)/shard_map/conv_general_dilated | solution.py:106
  99.4 16.1 %fusion.35 = f32[32,64,256]{2,0,1:T(8,128)} fusion(bf16[1,32,1087]{1,0,2:T(2,128)(2,1)S(1)} %copy.87, bf16[1,256,1024]{1,2,0:T(8,128)(2,1)S(1)} %fusion.53), kind=kOutput, calls=%fused_computation.40 | convolution fusion | flops 1073741824 | bytes 2691008 | tf_op jit(solution)/shard_map/conv_general_dilated | solution.py:122
  117.2 2.5 copy.89
  119.7 4.8 %all-to-all-start.1 = ((f32[8,256,256]{2,1,0:T(8,128)}), f32[8,256,256]{2,1,0:T(8,128)S(1)}, u32[]{:S(2)}, u32[]{:S(2)}) async-start(f32[8,256,256]{2,1,0:T(8,128)} %bitcast.115), calls=%async_computation.1 | async-start | bytes 4194304 | tf_op jit(solution)/shard_map/all_to_all | solution.py:84
  125.3 25.5 %all-to-all-done.1 = f32[8,256,256]{2,1,0:T(8,128)S(1)} async-done(((f32[8,256,256]{2,1,0:T(8,128)}), f32[8,256,256]{2,1,0:T(8,128)S(1)}, u32[]{:S(2)}, u32[]{:S(2)}) %all-to-all-start.1) | async-done | bytes 2097184 | tf_op jit(solution)/shard_map/all_to_all | solution.py:84
  152.8 3.1 collective-permute-done.8
  156.2 30.7 %all_to_all.50 = bf16[8,256,2,256]{3,1,2,0:T(8,128)(2,1)S(1)} all-to-all(bf16[8,256,2,256]{3,1,2,0:T(8,128)(2,1)S(1)} %broadcast_in_dim.64), channel_id=1, replica_groups=mesh['tm'=8,'neuron'=8,'motif'=2] {'tm'}, dimensions={0} | all-to-all | bytes 4194304 | tf_op jit(solution)/shard_map/all_to_all | solution.py:90
  187.9 3.0 fusion.15
  193.2 3.1 collective-permute-start.9
  200.7 10.5 %convolution_select_fusion = f32[8,136,32]{2,0,1:T(8,128)} fusion(bf16[32,64,256]{2,1,0:T(8,128)(2,1)S(1)} %bitcast.126, bf16[256,1,7,63]{0,2,3,1:T(8,128)(2,1)S(1)} %slice.69, bf16[256,1,8,136]{0,2,3,1:T(8,128)(2,1)S(1)} %copy.95, pred[8,136]{0,1:T(8,128)(4,1)S(1)} %copy-done.18), kind=kOutput, calls=%fused_computation.21 | convolution fusion | flops 1143330816 | bytes 1971776 | tf_op jit(solution)/shard_map/conv_general_dilated | solution.py:114
  213.6 22.6 %all_to_all.51 = f32[8,32,1088]{2,1,0:T(8,128)} all-to-all(f32[8,32,1088]{2,1,0:T(8,128)S(1)} %broadcast_in_dim.66), channel_id=1, replica_groups=mesh['tm'=8,'neuron'=8,'motif'=2] {'neuron'}, dimensions={0} | all-to-all | bytes 2228224 | tf_op jit(solution)/shard_map/all_to_all | solution.py:97
  239.4 3.0 collective-permute-start.10
  246.6 4.7 %all-to-all-start.6 = ((f32[8,1,256]{2,1,0:T(1,128)}), f32[8,1,256]{2,1,0:T(1,128)}, u32[]{:S(2)}, u32[]{:S(2)}) async-start(f32[8,1,256]{2,1,0:T(1,128)} %all_to_all.41), calls=%async_computation.6 | async-start | bytes 16384 | tf_op jit(solution)/shard_map/all_to_all | solution.py:84
  255.3 4.0 %fusion.21 = f32[8,136,256]{2,0,1:T(8,128)S(1)} fusion(bf16[64,64,256]{2,1,0:T(8,128)(2,1)S(1)} %bitcast.114, pred[8,136]{0,1:T(8,128)(4,1)} %constant.49, bf16[64,1,7,63]{0,2,3,1:T(8,128)(2,1)S(1)} %slice.75, bf16[64,1,8,136]{0,2,3,1:T(8,128)(2,1)} %copy.99), kind=kOutput, calls=%fused_computation.20 | convolution fusion | flops 2282869760 | bytes 3408064 | tf_op jit(solution)/shard_map/conv_general_dilated | solution.py:106
  260.7 15.9 %fusion.33 = f32[32,64,256]{2,0,1:T(8,128)} fusion(bf16[1,32,1087]{1,0,2:T(2,128)(2,1)S(1)} %copy-done.9, bf16[1,256,1024]{1,2,0:T(8,128)(2,1)S(1)} %fusion.54), kind=kOutput, calls=%fused_computation.38 | convolution fusion | flops 1073741824 | bytes 2691008 | tf_op jit(solution)/shard_map/conv_general_dilated | solution.py:122
  278.3 2.5 copy.104
  280.9 4.8 %all-to-all-start.5 = ((f32[8,256,256]{2,1,0:T(8,128)}), f32[8,256,256]{2,1,0:T(8,128)S(1)}, u32[]{:S(2)}, u32[]{:S(2)}) async-start(f32[8,256,256]{2,1,0:T(8,128)} %bitcast.116), calls=%async_computation.5 | async-start | bytes 4194304 | tf_op jit(solution)/shard_map/all_to_all | solution.py:84
  286.4 25.4 %all-to-all-done.5 = f32[8,256,256]{2,1,0:T(8,128)S(1)} async-done(((f32[8,256,256]{2,1,0:T(8,128)}), f32[8,256,256]{2,1,0:T(8,128)S(1)}, u32[]{:S(2)}, u32[]{:S(2)}) %all-to-all-start.5) | async-done | bytes 2097184 | tf_op jit(solution)/shard_map/all_to_all | solution.py:84
  313.3 29.6 %all_to_all.52 = f32[8,256,256]{2,1,0:T(8,128)S(1)} all-to-all(f32[8,256,256]{2,1,0:T(8,128)S(1)} %broadcast_in_dim.70), channel_id=1, replica_groups=mesh['tm'=8,'neuron'=8,'motif'=2] {'tm'}, dimensions={0} | all-to-all | bytes 4194304 | tf_op jit(solution)/shard_map/all_to_all | solution.py:90
  (143 shorter events, 45.5 us)
Async XLA Ops:
  0.6 5.5 %copy-start.10 = (f32[32,1024]{1,0:T(8,128)S(1)}, f32[32,1024]{1,0:T(8,128)}, u32[]{:S(2)}) copy-start(f32[32,1024]{1,0:T(8,128)} %param.5) | copy-start | bytes 393220
  0.6 13.1 %copy-start.5 = (s32[256,1024]{1,0:T(8,128)S(1)}, s32[256,1024]{1,0:T(8,128)}, u32[]{:S(2)}) copy-start(s32[256,1024]{1,0:T(8,128)} %param.3) | copy-start | bytes 3145732
  3.6 28.5 %collective-permute-start.3 = (bf16[32,64,256]{2,0,1:T(8,128)(2,1)S(1)}, bf16[32,64,256]{2,0,1:T(8,128)(2,1)}, u32[]{:S(2)}, u32[]{:S(2)}) collective-permute-start(bf16[32,64,256]{2,0,1:T(8,128)(2,1)S(1)} %get-tuple-element.3), channel_id=1, source_target_pairs={{0,1},{1,0},{2,3},{3,2},{4,5},{5,4},{6,7},{7,6},{8,9},{9,8},{10,11... | collective-permute-start | bytes 3145736 | tf_op jit(solution)/shard_map/ppermute | solution.py:19
  6.2 25.1 %collective-permute-start.2 = (bf16[32,1024]{1,0:T(8,128)(2,1)S(1)}, bf16[32,1024]{1,0:T(8,128)(2,1)S(1)}, u32[]{:S(2)}, u32[]{:S(2)}) collective-permute-start(bf16[32,1024]{1,0:T(8,128)(2,1)S(1)} %convert_element_type.40), channel_id=1, source_target_pairs={{0,1},{1,0},{2,3},{3,2},{4,5},{5,4},{6,7},{7,6},{8,9},{9,8},{10,11... | collective-permute-start | bytes 196616 | tf_op jit(solution)/shard_map/ppermute | solution.py:19
  6.3 24.9 %collective-permute-start.1 = (bf16[32,63]{1,0:T(8,128)(2,1)S(1)}, bf16[32,63]{1,0:T(8,128)(2,1)S(1)}, u32[]{:S(2)}, u32[]{:S(2)}) collective-permute-start(bf16[32,63]{1,0:T(8,128)(2,1)S(1)} %slice.56), channel_id=1, source_target_pairs={{0,17},{1,16},{16,33},{17,32},{32,49},{33,48},{48,65},{49,64},{64,... | collective-permute-start | bytes 12104 | tf_op jit(solution)/shard_map/ppermute | solution.py:78
  11.8 19.5 %collective-permute-start = (bf16[32,63]{1,0:T(8,128)(2,1)S(1)}, bf16[32,63]{1,0:T(8,128)(2,1)S(1)}, u32[]{:S(2)}, u32[]{:S(2)}) collective-permute-start(bf16[32,63]{1,0:T(8,128)(2,1)S(1)} %slice.56), channel_id=1, source_target_pairs={{0,16},{16,32},{32,48},{48,64},{64,80},{80,96},{96,112},{1,17},{17... | collective-permute-start | bytes 12104 | tf_op jit(solution)/shard_map/ppermute | solution.py:14
  14.1 85.1 %copy-start = (s32[256,1024]{0,1:T(8,128)}, s32[256,1024]{0,1:T(8,128)S(1)}, u32[]{:S(2)}) copy-start(s32[256,1024]{0,1:T(8,128)S(1)} %copy.75) | copy-start | bytes 3145732
  36.5 5.2 %collective-permute-start.4 = (bf16[256,63]{0,1:T(8,128)(2,1)S(1)}, bf16[256,63]{0,1:T(8,128)(2,1)S(1)}, u32[]{:S(2)}, u32[]{:S(2)}) collective-permute-start(bf16[256,63]{0,1:T(8,128)(2,1)S(1)} %slice.59), channel_id=1, source_target_pairs={{16,0},{32,16},{48,32},{64,48},{80,64},{96,80},{112,96},{17,1},{33... | collective-permute-start | bytes 96776 | tf_op jit(solution)/shard_map/ppermute | solution.py:14
  53.5 24.2 %all-to-all-start = ((f32[8,32,1088]{2,1,0:T(8,128)}), f32[8,32,1088]{2,1,0:T(8,128)S(1)}, u32[]{:S(2)}, u32[]{:S(2)}) async-start(f32[8,32,1088]{2,1,0:T(8,128)} %broadcast_in_dim.28), calls=%async_computation | async-start | bytes 2359296 | tf_op jit(solution)/shard_map/all_to_all | solution.py:97
  79.3 15.6 %copy-start.17 = (pred[8,136]{0,1:T(8,128)(4,1)S(1)}, pred[8,136]{0,1:T(8,128)(4,1)}, u32[]{:S(2)}) copy-start(pred[8,136]{0,1:T(8,128)(4,1)} %constant.49) | copy-start | bytes 3268
  79.4 8.1 %collective-permute-start.5 = (bf16[32,63]{1,0:T(8,128)(2,1)S(1)}, bf16[32,63]{1,0:T(8,128)(2,1)S(1)}, u32[]{:S(2)}, u32[]{:S(2)}) collective-permute-start(bf16[32,63]{1,0:T(8,128)(2,1)S(1)} %slice.64), channel_id=1, source_target_pairs={{0,16},{16,32},{32,48},{48,64},{64,80},{80,96},{96,112},{1,17},{17... | collective-permute-start | bytes 12104 | tf_op jit(solution)/shard_map/ppermute | solution.py:14
  84.0 4.5 %copy-start.19 = (s32[64]{0:T(128)}, s32[64]{0:T(128)S(1)}, u32[]{:S(2)}) copy-start(s32[64]{0:T(128)S(1)} %get-tuple-element.12) | copy-start | bytes 772
  84.0 4.5 %copy-start.21 = (s32[64]{0:T(128)}, s32[64]{0:T(128)S(1)}, u32[]{:S(2)}) copy-start(s32[64]{0:T(128)S(1)} %get-tuple-element.13) | copy-start | bytes 772
  84.0 10.1 %collective-permute-start.6 = (bf16[32,63]{1,0:T(8,128)(2,1)S(1)}, bf16[32,63]{1,0:T(8,128)(2,1)S(1)}, u32[]{:S(2)}, u32[]{:S(2)}) collective-permute-start(bf16[32,63]{1,0:T(8,128)(2,1)S(1)} %slice.64), channel_id=1, source_target_pairs={{0,17},{1,16},{16,33},{17,32},{32,49},{33,48},{48,65},{49,64},{64,... | collective-permute-start | bytes 12104 | tf_op jit(solution)/shard_map/ppermute | solution.py:78
  86.7 7.4 %collective-permute-start.7 = (bf16[32,1024]{1,0:T(8,128)(2,1)S(1)}, bf16[32,1024]{1,0:T(8,128)(2,1)S(1)}, u32[]{:S(2)}, u32[]{:S(2)}) collective-permute-start(bf16[32,1024]{1,0:T(8,128)(2,1)S(1)} %get-tuple-element.8), channel_id=1, source_target_pairs={{0,1},{1,0},{2,3},{3,2},{4,5},{5,4},{6,7},{7,6},{8,9},{9,8},{10,11... | collective-permute-start | bytes 196616 | tf_op jit(solution)/shard_map/ppermute | solution.py:19
  88.5 31.2 %all-to-all-start.2 = ((f32[8,1,256]{2,1,0:T(1,128)}), f32[8,1,256]{2,1,0:T(1,128)}, u32[]{:S(2)}, u32[]{:S(2)}) async-start(f32[8,1,256]{2,1,0:T(1,128)} %all_to_all.40), calls=%async_computation.2 | async-start | bytes 16384 | tf_op jit(solution)/shard_map/all_to_all | solution.py:84
  94.9 3.9 %copy-start.7 = (bf16[64,1,8,136]{0,2,3,1:T(8,128)(2,1)}, bf16[64,1,8,136]{0,2,3,1:T(8,128)(2,1)S(1)}, u32[]{:S(2)}) copy-start(bf16[64,1,8,136]{0,2,3,1:T(8,128)(2,1)S(1)} %copy.85) | copy-start | bytes 417796
  119.7 31.0 %all-to-all-start.1 = ((f32[8,256,256]{2,1,0:T(8,128)}), f32[8,256,256]{2,1,0:T(8,128)S(1)}, u32[]{:S(2)}, u32[]{:S(2)}) async-start(f32[8,256,256]{2,1,0:T(8,128)} %bitcast.115), calls=%async_computation.1 | async-start | bytes 4194304 | tf_op jit(solution)/shard_map/all_to_all | solution.py:84
  125.3 30.7 %copy-start.13 = (f32[256]{0:T(256)}, f32[256]{0:T(256)S(1)}, u32[]{:S(2)}) copy-start(f32[256]{0:T(256)S(1)} %reduce_sum.77) | copy-start | bytes 3076
  150.9 5.3 %copy-start.2 = (f32[256,256]{1,0:T(8,128)}, f32[256,256]{1,0:T(8,128)S(1)}, u32[]{:S(2)}) copy-start(f32[256,256]{1,0:T(8,128)S(1)} %reduce_sum.76) | copy-start | bytes 786436
  152.1 3.9 %collective-permute-start.8 = (bf16[256,256]{1,0:T(8,128)(2,1)S(1)}, bf16[256,256]{1,0:T(8,128)(2,1)S(1)}, u32[]{:S(2)}, u32[]{:S(2)}) collective-permute-start(bf16[256,256]{1,0:T(8,128)(2,1)S(1)} %fusion.117), channel_id=1, source_target_pairs={{0,1},{1,0},{2,3},{3,2},{4,5},{5,4},{6,7},{7,6},{8,9},{9,8},{10,11... | collective-permute-start | bytes 393224 | tf_op jit(solution)/shard_map/ppermute | solution.py:19
  193.2 5.2 %collective-permute-start.9 = (bf16[256,63]{0,1:T(8,128)(2,1)S(1)}, bf16[256,63]{0,1:T(8,128)(2,1)S(1)}, u32[]{:S(2)}, u32[]{:S(2)}) collective-permute-start(bf16[256,63]{0,1:T(8,128)(2,1)S(1)} %slice.68), channel_id=1, source_target_pairs={{16,0},{32,16},{48,32},{64,48},{80,64},{96,80},{112,96},{17,1},{33... | collective-permute-start | bytes 96776 | tf_op jit(solution)/shard_map/ppermute | solution.py:14
  213.6 24.0 %copy-start.15 = (s32[1024]{0:T(1024)S(1)}, s32[1024]{0:T(1024)}, u32[]{:S(2)}) copy-start(s32[1024]{0:T(1024)} %iota_add_fusion) | copy-start | bytes 12292
  213.6 32.0 %copy-start.20 = (s32[64]{0:T(128)S(1)}, s32[64]{0:T(128)}, u32[]{:S(2)}) copy-start(s32[64]{0:T(128)} %copy-done.19) | copy-start | bytes 772
  213.6 32.0 %copy-start.22 = (s32[64]{0:T(128)S(1)}, s32[64]{0:T(128)}, u32[]{:S(2)}) copy-start(s32[64]{0:T(128)} %copy-done.21) | copy-start | bytes 772
  239.4 6.2 %collective-permute-start.10 = (bf16[32,63]{1,0:T(8,128)(2,1)S(1)}, bf16[32,63]{1,0:T(8,128)(2,1)S(1)}, u32[]{:S(2)}, u32[]{:S(2)}) collective-permute-start(bf16[32,63]{1,0:T(8,128)(2,1)S(1)} %slice.74), channel_id=1, source_target_pairs={{0,16},{16,32},{32,48},{48,64},{64,80},{80,96},{96,112},{1,17},{17... | collective-permute-start | bytes 12104 | tf_op jit(solution)/shard_map/ppermute | solution.py:14
  242.4 10.4 %collective-permute-start.11 = (bf16[32,63]{1,0:T(8,128)(2,1)S(1)}, bf16[32,63]{1,0:T(8,128)(2,1)S(1)}, u32[]{:S(2)}, u32[]{:S(2)}) collective-permute-start(bf16[32,63]{1,0:T(8,128)(2,1)S(1)} %slice.74), channel_id=1, source_target_pairs={{0,17},{1,16},{16,33},{17,32},{32,49},{33,48},{48,65},{49,64},{64,... | collective-permute-start | bytes 12104 | tf_op jit(solution)/shard_map/ppermute | solution.py:78
  244.7 8.1 %collective-permute-start.12 = (bf16[32,1024]{1,0:T(8,128)(2,1)S(1)}, bf16[32,1024]{1,0:T(8,128)(2,1)S(1)}, u32[]{:S(2)}, u32[]{:S(2)}) collective-permute-start(bf16[32,1024]{1,0:T(8,128)(2,1)S(1)} %get-tuple-element.10), channel_id=1, source_target_pairs={{0,1},{1,0},{2,3},{3,2},{4,5},{5,4},{6,7},{7,6},{8,9},{9,8},{10,11... | collective-permute-start | bytes 196616 | tf_op jit(solution)/shard_map/ppermute | solution.py:19
  246.6 34.3 %all-to-all-start.6 = ((f32[8,1,256]{2,1,0:T(1,128)}), f32[8,1,256]{2,1,0:T(1,128)}, u32[]{:S(2)}, u32[]{:S(2)}) async-start(f32[8,1,256]{2,1,0:T(1,128)} %all_to_all.41), calls=%async_computation.6 | async-start | bytes 16384 | tf_op jit(solution)/shard_map/all_to_all | solution.py:84
  280.9 31.0 %all-to-all-start.5 = ((f32[8,256,256]{2,1,0:T(8,128)}), f32[8,256,256]{2,1,0:T(8,128)S(1)}, u32[]{:S(2)}, u32[]{:S(2)}) async-start(f32[8,256,256]{2,1,0:T(8,128)} %bitcast.116), calls=%async_computation.5 | async-start | bytes 4194304 | tf_op jit(solution)/shard_map/all_to_all | solution.py:84
  285.7 26.4 %copy-start.3 = (f32[256,256]{1,0:T(8,128)S(1)}, f32[256,256]{1,0:T(8,128)}, u32[]{:S(2)}) copy-start(f32[256,256]{1,0:T(8,128)} %copy-done.2) | copy-start | bytes 786436
  285.7 26.4 %copy-start.14 = (f32[256]{0:T(256)S(1)}, f32[256]{0:T(256)}, u32[]{:S(2)}) copy-start(f32[256]{0:T(256)} %copy-done.13) | copy-start | bytes 3076
  (9 other events, 11.9 us)
